TPU v7x, 256 devices: a whole 4x4x8 slice. The times are simulated.
256 devices in a mesh: dp: 8 (over x, core), expert: 32 (over y, z).
Axes of the slice: x: 4, y: 4, z: 8, core: 2. Of those that a mesh axis runs over, the one named last changes fastest.
Arguments:
- tokens: bfloat16 [32768, 2048], P(('dp', 'expert')), may hold values from -6 to 6
- cotangent: bfloat16 [32768, 2048], P(('dp', 'expert')), may hold values from -6 to 6
- router_logits: float32 [32768, 2], P(('dp', 'expert')), may hold values from -5 to 5
- expert_ids: int32 [32768, 2], P(('dp', 'expert')), may hold values from 0 to 31, all different within a row; in each aligned block of 128 rows (0 to 127, 128 to 255, ...) at most 14 rows name the same one
- w_in: bfloat16 [32, 2048, 1536], P('expert', 'dp'), may hold values from -0.125 to 0.125
- w_out: bfloat16 [32, 768, 2048], P('expert', 'dp'), may hold values from -0.21875 to 0.21875
Outputs:
- mixed: bfloat16 [32768, 2048], P(('dp', 'expert'))
- d_tokens: bfloat16 [32768, 2048], P(('dp', 'expert'))
- d_logits: float32 [32768, 2], P(('dp', 'expert'))
- grad_in: float32 [32, 2048, 1536], P('expert', 'dp')
- grad_out: float32 [32, 768, 2048], P('expert', 'dp')
Inputs may be any that keep to these rules, and one draw needn't show every extreme that they name: `expert_ids`: the 2 experts of a token differ; among the tokens of one device, no expert is chosen more than 14 times, and some expert is chosen exactly 14 times by some device.
All inputs are finite; a program needn't handle non-finite values.
Results may differ from a plain program's by a relative error of at most 0.015.
Values may be sent and summed in bfloat16 or wider, within the bound.
No kernel may reach another device: no remote copies, remote signals or barrier semaphores. Data moves between devices by JAX's collectives and lax.ppermute only.
A program may use at most 128 MiB of HBM per device.

v0:
```python
import jax
import jax.numpy as jnp
from jax import lax
from jax.sharding import PartitionSpec as P


def contract_rows(left, right):
    return lax.dot_general(
        left, right, (((0,), (0,)), ((), ())), preferred_element_type=jnp.float32
    )


def contract_cols(left, right):
    return lax.dot_general(
        left, right, (((1,), (1,)), ((), ())), preferred_element_type=jnp.float32
    )


def local(tokens, cotangent, router_logits, expert_ids, w_in, w_out):
    f32 = jnp.float32
    tok_rows, width = tokens.shape
    top = expert_ids.shape[1]
    experts = lax.axis_size("expert")
    capacity = 7 * tok_rows * top // (4 * experts)
    gathered_in, gathered_out = (
        lax.all_gather(w_in, "dp", axis=1, tiled=True),
        lax.all_gather(w_out, "dp", axis=1, tiled=True),
    )
    in_full = gathered_in[0]
    out_full = gathered_out[0]
    ff_units = in_full.shape[1] // 2
    flat_ids = expert_ids.reshape(-1)
    onehot = (flat_ids[:, None] == jnp.arange(experts, dtype=jnp.int32)[None, :]).astype(jnp.int32)
    before = jnp.cumsum(onehot, axis=0) - onehot
    position = jnp.sum(before * onehot, axis=1)
    slot_flat = flat_ids * capacity + position
    select = (
        jnp.arange(experts * capacity, dtype=jnp.int32)[:, None] == slot_flat[None, :]
    ).astype(jnp.bfloat16)
    repeated = jnp.repeat(tokens, top, axis=0)
    outgoing = jnp.dot(select, repeated, preferred_element_type=f32).astype(jnp.bfloat16)
    outgoing = outgoing.reshape(experts, capacity, width)
    piece = lax.all_to_all(outgoing, "expert", split_axis=0, concat_axis=0, tiled=True)
    joined = jnp.einsum("erd,df->erf", piece, in_full, preferred_element_type=f32)
    arrived_rows = piece.reshape(-1, width)
    joined = joined.reshape(-1, 2 * ff_units)
    gate_part = joined[:, :ff_units]
    up_part = joined[:, ff_units:]
    sigma = 1.0 / (1.0 + jnp.exp(-gate_part))
    silu = gate_part * sigma
    hidden = (silu * up_part).astype(jnp.bfloat16)
    results = jnp.dot(hidden, out_full, preferred_element_type=f32).astype(jnp.bfloat16)
    returned = lax.all_to_all(
        results.reshape(experts, capacity, width), "expert", split_axis=0, concat_axis=0, tiled=True
    )
    picked = contract_rows(select, returned.reshape(-1, width)).reshape(tok_rows, top, width)
    diffs = router_logits[:, None, :] - router_logits[:, :, None]
    gates = 1.0 / jnp.sum(jnp.exp(diffs), axis=-1)
    mixed = jnp.einsum("tk,tkd->td", gates, picked).astype(jnp.bfloat16)
    upstream = cotangent.astype(f32)
    d_gate = jnp.einsum("td,tkd->tk", upstream, picked)
    d_logits = gates * (d_gate - jnp.sum(gates * d_gate, axis=-1, keepdims=True))
    d_picks = (gates[:, :, None] * upstream[:, None, :]).astype(jnp.bfloat16).reshape(-1, width)
    d_outgoing = jnp.dot(select, d_picks, preferred_element_type=f32).astype(jnp.bfloat16)
    d_arrived = lax.all_to_all(
        d_outgoing.reshape(experts, capacity, width),
        "expert",
        split_axis=0,
        concat_axis=0,
        tiled=True,
    )
    d_arrived = d_arrived.reshape(-1, width)
    d_hidden = contract_cols(d_arrived, out_full)
    grad_down = contract_rows(hidden, d_arrived)
    d_joined = jnp.concatenate(
        [d_hidden * up_part * sigma * (1.0 + gate_part * (1.0 - sigma)), d_hidden * silu], axis=1
    ).astype(jnp.bfloat16)
    grad_up = contract_rows(arrived_rows, d_joined)
    up_share, down_share = (
        lax.psum_scatter(
            grad_up.astype(jnp.bfloat16), "dp", scatter_dimension=0, tiled=True
        ).astype(jnp.float32),
        lax.psum_scatter(
            grad_down.astype(jnp.bfloat16), "dp", scatter_dimension=0, tiled=True
        ).astype(jnp.float32),
    )
    d_rows = contract_cols(d_joined, in_full).astype(jnp.bfloat16)
    d_back = lax.all_to_all(
        d_rows.reshape(experts, capacity, width), "expert", split_axis=0, concat_axis=0, tiled=True
    )
    d_picked = contract_rows(select, d_back.reshape(-1, width)).reshape(tok_rows, top, width)
    d_tokens = jnp.sum(d_picked, axis=1).astype(jnp.bfloat16)
    return (mixed, d_tokens, d_logits, up_share[None], down_share[None])


def solution(mesh):
    placed = (
        P(("dp", "expert"), None),
        P(("dp", "expert"), None),
        P(("dp", "expert"), None),
        P(("dp", "expert"), None),
        P("expert", "dp", None),
        P("expert", "dp", None),
    )
    return jax.shard_map(
        local,
        mesh=mesh,
        in_specs=placed,
        out_specs=(
            P(("dp", "expert"), None),
            P(("dp", "expert"), None),
            P(("dp", "expert"), None),
            P("expert", "dp", None),
            P("expert", "dp", None),
        ),
        check_vma=False,
    )
```

profile of v0, /device:TPU:1, one launch (start us, length us, event | category | flops | bytes accessed | tf_op | source)
XLA Modules:
  0.0 324.9 jit_solution(16202993039292374891)
XLA Ops:
  7.2 0.7 all-gather.3.cloned.1.call-update
  8.0 0.7 all-gather.5.cloned.1.call-update
  8.7 0.8 copy.21
  9.7 0.6 reduce-window.6
  10.6 0.6 broadcast_in_dim.23
  11.2 0.4 reshape.121
  11.8 1.9 convolution_convert_fusion.3
  13.6 2.5 reshape.122
  16.1 59.1 %all_to_all.20 = bf16[32,14,2048]{2,1,0:T(8,128)(2,1)} all-to-all(bf16[32,14,2048]{2,1,0:T(8,128)(2,1)S(1)} %reshape.122), channel_id=1, replica_groups=mesh['dp'=8,'expert'=32] {'expert'}, dimensions={0} | all-to-all | bytes 3670016 | tf_op jit(solution)/shard_map/all_to_all | solution.py:43
  75.2 2.6 dot_general.39
  77.8 5.8 %fusion.2 = f32[448,1536]{1,0:T(8,128)S(1)} fusion(bf16[448,2048]{1,0:T(8,128)(2,1)S(1)} %dot_general.39, bf16[1,2048,1536]{2,1,0:T(8,128)(2,1)} %all-gather.3.cloned.1.call-done), kind=kOutput, calls=%fused_computation.3 | convolution fusion | flops 2818572288 | bytes 10878976 | tf_op jit(solution)/shard_map/erd,df->erf/dot_general | solution.py:44
  83.6 1.5 copy-done
  85.1 0.4 multiply_convert_fusion.3
  85.5 4.1 %all-gather.5.cloned.1.call-done = bf16[1,768,2048]{2,1,0:T(8,128)(2,1)} async-done(((bf16[1,96,2048]{2,1,0:T(8,128)(2,1)}), bf16[1,768,2048]{2,1,0:T(8,128)(2,1)}) %all-gather.5.cloned.1.call-update) | async-done | bytes 3145744 | tf_op jit(solution)/shard_map/all_gather | solution.py:27
  89.6 3.5 %fusion.8 = bf16[448,2048]{1,0:T(8,128)(2,1)S(1)} fusion(bf16[448,768]{1,0:T(8,128)(2,1)S(1)} %multiply_convert_fusion.3, bf16[1,768,2048]{2,1,0:T(8,128)(2,1)} %all-gather.5.cloned.1.call-done), kind=kOutput, calls=%fused_computation.12 | convolution fusion | flops 1410203648 | bytes 5668864 | tf_op jit(solution)/shard_map/dot_general | solution.py:52
  93.1 1.6 reshape.123
  94.7 9.8 %all-to-all-start.1 = ((bf16[32,14,2048]{2,1,0:T(8,128)(2,1)}), bf16[32,14,2048]{2,1,0:T(8,128)(2,1)}, u32[]{:S(2)}, u32[]{:S(2)}) async-start(bf16[32,14,2048]{2,1,0:T(8,128)(2,1)} %reshape.123), calls=%async_computation.1 | async-start | bytes 4194304 | tf_op jit(solution)/shard_map/all_to_all | solution.py:53
  105.1 0.3 copy.24
  105.4 2.4 mul.62
  107.8 2.7 mul.63
  110.6 43.0 %all-to-all-done.1 = bf16[32,14,2048]{2,1,0:T(8,128)(2,1)} async-done(((bf16[32,14,2048]{2,1,0:T(8,128)(2,1)}), bf16[32,14,2048]{2,1,0:T(8,128)(2,1)}, u32[]{:S(2)}, u32[]{:S(2)}) %all-to-all-start.1) | async-done | bytes 1835040 | tf_op jit(solution)/shard_map/all_to_all | solution.py:53
  153.5 3.7 %reshape.131 = bf16[448,2048,1]{1,0,2:T(8,128)(2,1)} reshape(bf16[32,14,2048]{2,1,0:T(8,128)(2,1)} %all-to-all-done.1) | data formatting | bytes 3670016 | tf_op jit(solution)/shard_map/reshape | solution.py:56
  157.2 2.3 fusion.31
  159.5 1.0 copy-done.5
  160.4 2.3 fusion.14
  163.1 2.0 convolution_convert_fusion.2
  165.2 2.5 reshape.125
  167.7 54.5 %all_to_all.21 = bf16[32,14,2048]{2,1,0:T(8,128)(2,1)} all-to-all(bf16[32,14,2048]{2,1,0:T(8,128)(2,1)S(1)} %reshape.125), channel_id=1, replica_groups=mesh['dp'=8,'expert'=32] {'expert'}, dimensions={0} | all-to-all | bytes 3670016 | tf_op jit(solution)/shard_map/all_to_all | solution.py:65
  222.2 2.5 reshape.126
  224.7 1.2 copy-done.4
  225.9 3.5 %convolution_convert_fusion.1 = bf16[768,2048]{1,0:T(8,128)(2,1)} fusion(bf16[448,768]{1,0:T(8,128)(2,1)S(1)} %multiply_convert_fusion.3, bf16[448,2048]{1,0:T(8,128)(2,1)S(1)} %reshape.126), kind=kOutput, calls=%fused_computation.5 | convolution fusion | flops 1410859008 | bytes 5668864 | tf_op jit(solution)/shard_map/dot_general | solution.py:8
  229.4 0.3 reduce-scatter.3.cloned.1.call-start
  229.7 1.5 copy-done.1
  231.2 4.5 %multiply_convert_fusion.2 = (bf16[448,768]{1,0:T(8,128)(2,1)S(1)}, bf16[448,768]{1,0:T(8,128)(2,1)S(1)}) fusion(f32[448,1536]{1,0:T(8,128)S(1)} %copy-done.1, bf16[448,2048]{1,0:T(8,128)(2,1)} %copy-done.4, bf16[1,768,2048]{2,1,0:T(8,128)(2,1)} %all-gather.5.cloned.1.call-done), kind=kOutput, calls=%fused_computation.22 | convolution fusion | flops 1413758976 | bytes 9109504 | tf_op jit(solution)/shard_map/dot_general | solution.py:14
  235.7 0.8 copy-done.10
  236.8 5.6 %convolution_convert_fusion = bf16[2048,1536]{1,0:T(8,128)(2,1)} fusion(bf16[448,2048]{1,0:T(8,128)(2,1)S(1)} %copy-done.3, bf16[448,768]{1,0:T(8,128)(2,1)S(1)} %get-tuple-element.8, bf16[448,768]{1,0:T(8,128)(2,1)S(1)} %get-tuple-element.7), kind=kOutput, calls=%fused_computation | convolution fusion | flops 2824470528 | bytes 9502720 | tf_op jit(solution)/shard_map/dot_general | solution.py:8
  242.5 1.1 copy-done.11
  243.7 5.9 %fusion.11 = bf16[448,2048]{1,0:T(8,128)(2,1)S(1)} fusion(bf16[1,2048,1536]{2,1,0:T(8,128)(2,1)} %all-gather.3.cloned.1.call-done, bf16[448,768]{1,0:T(8,128)(2,1)S(1)} %copy-done.13, bf16[448,768]{1,0:T(8,128)(2,1)S(1)} %copy-done.11), kind=kOutput, calls=%fused_computation.13 | convolution fusion | flops 2822242304 | bytes 9502720 | tf_op jit(solution)/shard_map/dot_general | solution.py:14
  249.7 1.6 reshape.127
  251.3 8.6 %all-to-all-start.3 = ((bf16[32,14,2048]{2,1,0:T(8,128)(2,1)}), bf16[32,14,2048]{2,1,0:T(8,128)(2,1)S(1)}, u32[]{:S(2)}, u32[]{:S(2)}) async-start(bf16[32,14,2048]{2,1,0:T(8,128)(2,1)} %reshape.127), calls=%async_computation.3 | async-start | bytes 4194304 | tf_op jit(solution)/shard_map/all_to_all | solution.py:88
  260.1 1.3 fusion.16
  261.4 1.1 copy.41
  262.5 0.6 fusion.28
  263.1 46.2 %all-to-all-done.3 = bf16[32,14,2048]{2,1,0:T(8,128)(2,1)S(1)} async-done(((bf16[32,14,2048]{2,1,0:T(8,128)(2,1)}), bf16[32,14,2048]{2,1,0:T(8,128)(2,1)S(1)}, u32[]{:S(2)}, u32[]{:S(2)}) %all-to-all-start.3) | async-done | bytes 1835040 | tf_op jit(solution)/shard_map/all_to_all | solution.py:88
  309.2 1.5 reshape.134
  310.8 3.2 convolution_reduce_fusion
  314.0 1.9 bitcast_convert_fusion.2
  315.9 2.5 bitcast_convert_fusion.1
  (46 shorter events, 2.3 us)
Async XLA Ops:
  7.2 3.4 %copy-start.7 = (bf16[128,2048]{1,0:T(8,128)(2,1)S(1)}, bf16[128,2048]{1,0:T(8,128)(2,1)}, u32[]{:S(2)}) copy-start(bf16[128,2048]{1,0:T(8,128)(2,1)} %param.6) | copy-start | bytes 1572868
  7.2 70.6 %all-gather.3.cloned.1.call-start = ((), (), s32[]{:S(2)}) async-start(), calls=%async_computation.6 | async-start | bytes 7077888 | tf_op jit(solution)/shard_map/all_gather | solution.py:26
  7.9 81.7 %all-gather.5.cloned.1.call-start = ((), (), s32[]{:S(2)}) async-start(), calls=%async_computation.7 | async-start | bytes 3538944 | tf_op jit(solution)/shard_map/all_gather | solution.py:27
  77.7 5.8 %copy-start.2 = (bf16[448,2048]{1,0:T(8,128)(2,1)}, bf16[448,2048]{1,0:T(8,128)(2,1)S(1)}, u32[]{:S(2)}) copy-start(bf16[448,2048]{1,0:T(8,128)(2,1)S(1)} %dot_general.39) | copy-start | bytes 5505028
  83.5 1.5 copy-start
  94.7 10.7 %copy-start.8 = (bf16[128,2048]{1,0:T(8,128)(2,1)S(1)}, bf16[128,2048]{1,0:T(8,128)(2,1)}, u32[]{:S(2)}) copy-start(bf16[128,2048]{1,0:T(8,128)(2,1)} %param.7) | copy-start | bytes 1572868
  94.7 58.8 %all-to-all-start.1 = ((bf16[32,14,2048]{2,1,0:T(8,128)(2,1)}), bf16[32,14,2048]{2,1,0:T(8,128)(2,1)}, u32[]{:S(2)}, u32[]{:S(2)}) async-start(bf16[32,14,2048]{2,1,0:T(8,128)(2,1)} %reshape.123), calls=%async_computation.1 | async-start | bytes 4194304 | tf_op jit(solution)/shard_map/all_to_all | solution.py:53
  104.5 209.4 %reduce-scatter.5.cloned.1.call-start = ((), (), s32[]{:S(2)}) async-start(), calls=%async_computation.9 | async-start | bytes 3538944 | tf_op jit(solution)/shard_map/reduce_scatter | solution.py:83
  107.8 2.7 copy-start.9
  159.5 1.0 copy-start.5
  224.7 1.2 copy-start.4
  229.4 1.8 copy-start.1
  229.4 86.5 %reduce-scatter.3.cloned.1.call-start = ((), (), s32[]{:S(2)}) async-start(), calls=%async_computation.8 | async-start | bytes 7077888 | tf_op jit(solution)/shard_map/reduce_scatter | solution.py:80
  231.2 5.6 %copy-start.3 = (bf16[448,2048]{1,0:T(8,128)(2,1)S(1)}, bf16[448,2048]{1,0:T(8,128)(2,1)}, u32[]{:S(2)}) copy-start(bf16[448,2048]{1,0:T(8,128)(2,1)} %copy-done.2) | copy-start | bytes 5505028
  235.7 0.9 copy-start.10
  235.7 1.1 copy-start.12
  242.4 1.1 copy-start.11
  242.4 1.3 copy-start.13
  251.3 8.8 %copy-start.6 = (bf16[128,2,2048]{2,0,1:T(8,128)(2,1)S(1)}, bf16[128,2,2048]{2,0,1:T(8,128)(2,1)}, u32[]{:S(2)}) copy-start(bf16[128,2,2048]{2,0,1:T(8,128)(2,1)} %copy-done.5) | copy-start | bytes 3145732
  251.3 57.9 %all-to-all-start.3 = ((bf16[32,14,2048]{2,1,0:T(8,128)(2,1)}), bf16[32,14,2048]{2,1,0:T(8,128)(2,1)S(1)}, u32[]{:S(2)}, u32[]{:S(2)}) async-start(bf16[32,14,2048]{2,1,0:T(8,128)(2,1)} %reshape.127), calls=%async_computation.3 | async-start | bytes 4194304 | tf_op jit(solution)/shard_map/all_to_all | solution.py:88
Sparse Core Ops, SparseCore 0:
  9.8 47.5 all-gather.2
  59.2 30.3 all-gather.4
  229.6 35.2 reduce-scatter.4
  267.3 46.0 reduce-scatter.2
where the time goes:
time: 326 us; the launch traced here: 325 us
  blocking collectives  114 us (35%)
  waiting for transfers between devices  94.7 us (29%)
  matrix products  41.8 us (13%)
  local copies, waits for them, and re-layouts  35.5 us (11%)
  starting transfers between devices  19 us (6%)
  between operations  14 us (4%)
  other arithmetic  6.32 us (2%)
    all_to_all x1, blocking collectives, local(): lax.all_to_all(outgoing, 'expert', split_axis=0, concat_axis=0, tiled=True)  59.1 us
    all_to_all x1, blocking collectives, local(): lax.all_to_all(d_outgoing.reshape(experts, capacity, width), 'expert', sp...  54.5 us
    all_to_all x1, waiting for transfers between devices, local(): lax.all_to_all(d_rows.reshape(experts, capacity, width), 'expert', split_...  46.2 us
    all_to_all x1, waiting for transfers between devices, local(): lax.all_to_all(results.reshape(experts, capacity, width), 'expert', split...  43 us
    dot_general x4, matrix products, contract_rows(): lax.dot_general(left, right, (((0,), (0,)), ((), ())), preferred_element_...  14.6 us
    dot_general x2, matrix products, contract_cols(): lax.dot_general(left, right, (((1,), (1,)), ((), ())), preferred_element_...  10.5 us
    all_to_all x1, starting transfers between devices, local(): lax.all_to_all(results.reshape(experts, capacity, width), 'expert', split...  9.83 us
    all_to_all x1, starting transfers between devices, local(): lax.all_to_all(d_rows.reshape(experts, capacity, width), 'expert', split_...  8.62 us
  transfers between devices with their start and end apart: 6, of which 3 were waited for; matrix products, arithmetic and copies ran while one was open for 15% of the time, Pallas kernels for 0%

commit v1 on v0

v1 whole, which is shorter than its diff:
```python
import jax
import jax.numpy as jnp
from jax import lax
from jax.sharding import PartitionSpec as P


def contract_rows(left, right):
    return lax.dot_general(
        left, right, (((0,), (0,)), ((), ())), preferred_element_type=jnp.float32
    )


def contract_cols(left, right):
    return lax.dot_general(
        left, right, (((1,), (1,)), ((), ())), preferred_element_type=jnp.float32
    )


def local(tokens, cotangent, router_logits, expert_ids, w_in, w_out):
    f32 = jnp.float32
    bf16 = jnp.bfloat16
    tok_rows, width = tokens.shape
    top = expert_ids.shape[1]
    experts = lax.axis_size("expert")
    capacity = 7 * tok_rows * top // (4 * experts)
    gathered_in, gathered_out = (
        lax.all_gather(w_in, "dp", axis=1, tiled=True),
        lax.all_gather(w_out, "dp", axis=1, tiled=True),
    )
    in_full = gathered_in[0]
    out_full = gathered_out[0]
    ff_units = in_full.shape[1] // 2
    flat_ids = expert_ids.reshape(-1)
    onehot = (flat_ids[:, None] == jnp.arange(experts, dtype=jnp.int32)[None, :]).astype(jnp.int32)
    before = jnp.cumsum(onehot, axis=0) - onehot
    position = jnp.sum(before * onehot, axis=1)
    slot_flat = flat_ids * capacity + position
    select = (
        jnp.arange(experts * capacity, dtype=jnp.int32)[:, None] == slot_flat[None, :]
    ).astype(bf16)
    diffs = router_logits[:, None, :] - router_logits[:, :, None]
    gates = 1.0 / jnp.sum(jnp.exp(diffs), axis=-1)
    upstream = cotangent.astype(f32)
    repeated = jnp.repeat(tokens, top, axis=0)
    d_picks = (gates[:, :, None] * upstream[:, None, :]).astype(bf16).reshape(-1, width)
    sendable = jnp.concatenate([repeated, d_picks], axis=1)
    outgoing = jnp.dot(select, sendable, preferred_element_type=f32).astype(bf16)
    arrived = lax.all_to_all(
        outgoing.reshape(experts, capacity, 2 * width), "expert", split_axis=0, concat_axis=0, tiled=True
    ).reshape(-1, 2 * width)
    piece = arrived[:, :width]
    d_arrived = arrived[:, width:]
    joined = jnp.dot(piece, in_full, preferred_element_type=f32)
    gate_part = joined[:, :ff_units]
    up_part = joined[:, ff_units:]
    sigma = 1.0 / (1.0 + jnp.exp(-gate_part))
    silu = gate_part * sigma
    hidden = (silu * up_part).astype(bf16)
    results = jnp.dot(hidden, out_full, preferred_element_type=f32).astype(bf16)
    d_hidden = contract_cols(d_arrived, out_full)
    grad_down = contract_rows(hidden, d_arrived)
    d_joined = jnp.concatenate(
        [d_hidden * up_part * sigma * (1.0 + gate_part * (1.0 - sigma)), d_hidden * silu], axis=1
    ).astype(bf16)
    grad_up = contract_rows(piece, d_joined)
    up_share, down_share = (
        lax.psum_scatter(grad_up.astype(bf16), "dp", scatter_dimension=0, tiled=True).astype(f32),
        lax.psum_scatter(grad_down.astype(bf16), "dp", scatter_dimension=0, tiled=True).astype(f32),
    )
    d_rows = contract_cols(d_joined, in_full).astype(bf16)
    back = jnp.concatenate([results, d_rows], axis=1)
    returned = lax.all_to_all(
        back.reshape(experts, capacity, 2 * width), "expert", split_axis=0, concat_axis=0, tiled=True
    ).reshape(-1, 2 * width)
    picked_both = contract_rows(select, returned).reshape(tok_rows, top, 2 * width)
    picked = picked_both[:, :, :width]
    d_picked = picked_both[:, :, width:]
    mixed = jnp.einsum("tk,tkd->td", gates, picked).astype(bf16)
    d_gate = jnp.einsum("td,tkd->tk", upstream, picked)
    d_logits = gates * (d_gate - jnp.sum(gates * d_gate, axis=-1, keepdims=True))
    d_tokens = jnp.sum(d_picked, axis=1).astype(bf16)
    return (mixed, d_tokens, d_logits, up_share[None], down_share[None])


def solution(mesh):
    placed = (
        P(("dp", "expert"), None),
        P(("dp", "expert"), None),
        P(("dp", "expert"), None),
        P(("dp", "expert"), None),
        P("expert", "dp", None),
        P("expert", "dp", None),
    )
    return jax.shard_map(
        local,
        mesh=mesh,
        in_specs=placed,
        out_specs=(
            P(("dp", "expert"), None),
            P(("dp", "expert"), None),
            P(("dp", "expert"), None),
            P("expert", "dp", None),
            P("expert", "dp", None),
        ),
        check_vma=False,
    )
```

time: 326 us -> 309 us (0.948); the launches traced: 325 us -> 304 us
  blocking collectives: 114 us -> 0 us
  waiting for transfers between devices: 94.7 us -> 183 us
  other arithmetic: 6.32 us -> 10.8 us
  starting transfers between devices: 19 us -> 22.4 us
    all_to_all x2 -> x0, blocking collectives: 114 us -> none  [the longest x1 59.1 us: local(): lax.all_to_all(outgoing, 'expert', split_axis=0, concat_axis=0, tiled=True)]
    all_to_all x2, waiting for transfers between devices: 89.1 us -> 176 us  [the longest x1 91.7 us: local(): lax.all_to_all(outgoing.reshape(experts, capacity, 2 * width), 'expert',...]
    reduce_scatter x2, waiting for transfers between devices: 0.01 us -> 5.49 us  [the longest x1 5.49 us: local(): lax.psum_scatter(grad_down.astype(bf16), 'dp', scatter_dimension=0, tiled...]
    unnamed x29 -> x25, local copies, waits for them, and re-layouts: 8.31 us -> 3.22 us
    all_gather x1, waiting for transfers between devices: 4.12 us -> 0.01 us  [local(): lax.all_gather(w_out, 'dp', axis=1, tiled=True)]
    reshape x7 -> x4, local copies, waits for them, and re-layouts: 15.9 us -> 20 us  [the longest x1 5.02 us: local(): back.reshape(experts, capacity, 2 * width)]
    all_to_all x2, starting transfers between devices: 18.5 us -> 22.1 us  [the longest x1 12.3 us: local(): lax.all_to_all(outgoing.reshape(experts, capacity, 2 * width), 'expert',...]
    dot_general x5 -> x4, matrix products: 14.4 us -> 15.8 us  [the longest x1 7.95 us: local(): joined = jnp.dot(piece, in_full, preferred_element_type=f32)]
  transfers between devices with their start and end apart: 6 -> 6, of which waited for: 3 -> 3; matrix products, arithmetic and copies ran while one was open for 15% -> 23% of each run, Pallas kernels for 0% -> 0%
where the time goes in v1:
time: 309 us; the launch traced here: 304 us
  waiting for transfers between devices  183 us (59%)
  matrix products  40.7 us (13%)
  local copies, waits for them, and re-layouts  33.1 us (11%)
  starting transfers between devices  22.4 us (7%)
  between operations  14 us (5%)
  other arithmetic  10.8 us (3%)
    all_to_all x1, waiting for transfers between devices, local(): lax.all_to_all(outgoing.reshape(experts, capacity, 2 * width), 'expert',...  91.7 us
    all_to_all x1, waiting for transfers between devices, local(): lax.all_to_all(back.reshape(experts, capacity, 2 * width), 'expert', spli...  84.8 us
    dot_general x3, matrix products, contract_rows(): lax.dot_general(left, right, (((0,), (0,)), ((), ())), preferred_element_...  14.1 us
    all_to_all x1, starting transfers between devices, local(): lax.all_to_all(outgoing.reshape(experts, capacity, 2 * width), 'expert',...  12.3 us
    all_to_all x1, starting transfers between devices, local(): lax.all_to_all(back.reshape(experts, capacity, 2 * width), 'expert', spli...  9.81 us
    dot_general x2, matrix products, contract_cols(): lax.dot_general(left, right, (((1,), (1,)), ((), ())), preferred_element_...  8.46 us
    dot_general x1, matrix products, local(): joined = jnp.dot(piece, in_full, preferred_element_type=f32)  7.95 us
  transfers between devices with their start and end apart: 6, of which 3 were waited for; matrix products, arithmetic and copies ran while one was open for 23% of the time, Pallas kernels for 0%

profile of v1, /device:TPU:1, one launch (start us, length us, event | category | flops | bytes accessed | tf_op | source)
XLA Modules:
  0.0 304.5 jit_solution(2566945622301600420)
XLA Ops:
  7.2 0.7 all-gather.3.cloned.1.call-update
  7.9 0.8 copy.20
  8.7 0.1 reshape.93
  8.8 0.1 eq.55
  9.0 2.1 mul.60
  11.1 2.5 mul.61
  13.6 0.1 copy.23
  13.7 0.1 div.18
  13.8 1.8 broadcast_in_dim.23
  15.7 1.2 reshape.95
  16.9 0.6 reduce-window.6
  17.5 0.2 slice_reduce_fusion.1
  17.7 0.1 fusion.32
  17.9 0.2 multiply_convert_fusion
  18.1 3.0 convolution_convert_fusion.1
  21.1 5.0 %reshape.96 = bf16[32,14,4096]{2,1,0:T(8,128)(2,1)} reshape(bf16[448,4096]{1,0:T(8,128)(2,1)} %convolution_convert_fusion.1) | data formatting | bytes 7340032 | tf_op jit(solution)/shard_map/reshape | solution.py:49
  26.1 12.3 %all-to-all-start = ((bf16[32,14,4096]{2,1,0:T(8,128)(2,1)}), bf16[32,14,4096]{2,1,0:T(8,128)(2,1)}, u32[]{:S(2)}, u32[]{:S(2)}) async-start(bf16[32,14,4096]{2,1,0:T(8,128)(2,1)} %reshape.96), calls=%async_computation | async-start | bytes 8388608 | tf_op jit(solution)/shard_map/all_to_all | solution.py:48
  38.4 0.7 all-gather.5.cloned.1.call-update
  39.2 91.7 %all-to-all-done = bf16[32,14,4096]{2,1,0:T(8,128)(2,1)} async-done(((bf16[32,14,4096]{2,1,0:T(8,128)(2,1)}), bf16[32,14,4096]{2,1,0:T(8,128)(2,1)}, u32[]{:S(2)}, u32[]{:S(2)}) %all-to-all-start) | async-done | bytes 3670048 | tf_op jit(solution)/shard_map/all_to_all | solution.py:48
  130.9 5.0 %reshape.97 = bf16[448,4096]{1,0:T(8,128)(2,1)} reshape(bf16[32,14,4096]{2,1,0:T(8,128)(2,1)} %all-to-all-done) | data formatting | bytes 7340032 | tf_op jit(solution)/shard_map/reshape | solution.py:50
  135.9 7.9 %fusion.2 = f32[448,1536]{1,0:T(8,128)} fusion(bf16[1,2048,1536]{2,1,0:T(8,128)(2,1)} %all-gather.3.cloned.1.call-done, bf16[448,4096]{1,0:T(8,128)(2,1)} %reshape.97), kind=kOutput, calls=%fused_computation.3 | convolution fusion | flops 2818572288 | bytes 10878976 | tf_op jit(solution)/shard_map/dot_general | solution.py:53
  143.8 5.4 %multiply_convert_fusion.2 = (bf16[448,768]{1,0:T(8,128)(2,1)S(1)}, bf16[448,768]{1,0:T(8,128)(2,1)S(1)}, bf16[448,768]{1,0:T(8,128)(2,1)S(1)}) fusion(f32[448,1536]{1,0:T(8,128)} %fusion.2, bf16[1,768,2048]{2,1,0:T(8,128)(2,1)} %all-gather.5.cloned.1.call-done, bf16[448,4096]{1,0:T(8,128)(2,1)} %reshape.97), kind=kOutput, calls=%fused_computation.29 | convolution fusion | flops 1414447104 | bytes 9797632 | tf_op jit(solution)/shard_map/dot_general | solution.py:14
  149.3 3.6 %convolution_convert_fusion.2 = bf16[768,2048]{1,0:T(8,128)(2,1)} fusion(bf16[448,768]{1,0:T(8,128)(2,1)S(1)} %get-tuple-element.7, bf16[448,4096]{1,0:T(8,128)(2,1)S(1)} %copy-done.3), kind=kOutput, calls=%fused_computation.7 | convolution fusion | flops 1410859008 | bytes 5668864 | tf_op jit(solution)/shard_map/dot_general | solution.py:8
  152.9 0.2 reduce-scatter.3.cloned.1.call-start
  153.1 7.2 %convolution_convert_fusion = bf16[2048,1536]{1,0:T(8,128)(2,1)} fusion(bf16[448,4096]{1,0:T(8,128)(2,1)} %reshape.97, bf16[448,768]{1,0:T(8,128)(2,1)S(1)} %get-tuple-element.6, bf16[448,768]{1,0:T(8,128)(2,1)S(1)} %get-tuple-element.5), kind=kOutput, calls=%fused_computation | convolution fusion | flops 2824470528 | bytes 9502720 | tf_op jit(solution)/shard_map/dot_general | solution.py:8
  160.4 3.6 %fusion.8 = bf16[448,2048]{1,0:T(8,128)(2,1)S(1)} fusion(bf16[448,768]{1,0:T(8,128)(2,1)S(1)} %get-tuple-element.7, bf16[1,768,2048]{2,1,0:T(8,128)(2,1)} %all-gather.5.cloned.1.call-done), kind=kOutput, calls=%fused_computation.12 | convolution fusion | flops 1410203648 | bytes 5668864 | tf_op jit(solution)/shard_map/dot_general | solution.py:59
  164.1 0.1 copy-done.7
  164.3 0.2 copy-done.9
  164.5 3.0 fusion.11
  167.5 2.0 pad_maximum_fusion
  169.5 5.0 %reshape.98 = bf16[32,14,4096]{2,1,0:T(8,128)(2,1)} reshape(bf16[448,4096]{1,0:T(8,128)(2,1)} %pad_maximum_fusion) | data formatting | bytes 7340032 | tf_op jit(solution)/shard_map/reshape | solution.py:73
  174.5 9.8 %all-to-all-start.1 = ((bf16[32,14,4096]{2,1,0:T(8,128)(2,1)}), bf16[32,14,4096]{2,1,0:T(8,128)(2,1)}, u32[]{:S(2)}, u32[]{:S(2)}) async-start(bf16[32,14,4096]{2,1,0:T(8,128)(2,1)} %reshape.98), calls=%async_computation.1 | async-start | bytes 8388608 | tf_op jit(solution)/shard_map/all_to_all | solution.py:72
  184.4 0.2 copy.25
  184.5 0.1 iota_compare_fusion
  184.7 0.2 eq.61
  184.9 5.5 %reduce-scatter.5.cloned.1.call-done = bf16[96,2048]{1,0:T(8,128)(2,1)} async-done(((bf16[768,2048]{1,0:T(8,128)(2,1)}), bf16[96,2048]{1,0:T(8,128)(2,1)}) %reduce-scatter.5.cloned.1.call-update) | async-done | bytes 393232 | tf_op jit(solution)/shard_map/reduce_scatter | solution.py:68
  190.4 1.9 bitcast_convert_fusion.2
  192.3 84.8 %all-to-all-done.1 = bf16[32,14,4096]{2,1,0:T(8,128)(2,1)} async-done(((bf16[32,14,4096]{2,1,0:T(8,128)(2,1)}), bf16[32,14,4096]{2,1,0:T(8,128)(2,1)}, u32[]{:S(2)}, u32[]{:S(2)}) %all-to-all-start.1) | async-done | bytes 3670048 | tf_op jit(solution)/shard_map/all_to_all | solution.py:72
  277.1 5.0 %reshape.102 = bf16[448,4096,1]{1,0,2:T(8,128)(2,1)} reshape(bf16[32,14,4096]{2,1,0:T(8,128)(2,1)} %all-to-all-done.1) | data formatting | bytes 7340032 | tf_op jit(solution)/shard_map/reshape | solution.py:74
  282.0 3.3 %fusion.27 = f32[128,2,4096]{2,0,1:T(8,128)S(1)} fusion(bf16[448,4096,1]{1,0,2:T(8,128)(2,1)} %reshape.102, pred[128,2,448]{2,1,0:T(4,128)(4,1)S(1)} %eq.61), kind=kOutput, calls=%fused_computation.37 | convolution fusion | flops 939524096 | bytes 7979008 | tf_op jit(solution)/shard_map/dot_general | solution.py:8
  285.4 1.9 copy-done
  287.3 0.1 slice.37
  287.4 1.3 fusion.23
  288.7 1.1 copy.41
  289.8 2.3 fusion.21
  292.2 2.7 slice_reduce_fusion
  294.9 0.6 fusion.35
  295.5 2.5 bitcast_convert_fusion.1
  (39 shorter events, 0.5 us)
Async XLA Ops:
  7.2 128.7 %all-gather.3.cloned.1.call-start = ((), (), s32[]{:S(2)}) async-start(), calls=%async_computation.4 | async-start | bytes 7077888 | tf_op jit(solution)/shard_map/all_gather | solution.py:27
  9.0 4.6 %copy-start.5 = (f32[128,2]{0,1:T(2,128)S(1)}, f32[128,2]{0,1:T(2,128)}, u32[]{:S(2)}) copy-start(f32[128,2]{0,1:T(2,128)} %param.8) | copy-start | bytes 3076
  13.5 4.3 %copy-start.1 = (f32[256,2048]{1,0:T(8,128)S(1)}, f32[256,2048]{1,0:T(8,128)}, u32[]{:S(2)}) copy-start(f32[256,2048]{1,0:T(8,128)} %mul.61) | copy-start | bytes 6291460
  16.9 1.2 copy-start.2
  26.1 104.8 %all-to-all-start = ((bf16[32,14,4096]{2,1,0:T(8,128)(2,1)}), bf16[32,14,4096]{2,1,0:T(8,128)(2,1)}, u32[]{:S(2)}, u32[]{:S(2)}) async-start(bf16[32,14,4096]{2,1,0:T(8,128)(2,1)} %reshape.96), calls=%async_computation | async-start | bytes 8388608 | tf_op jit(solution)/shard_map/all_to_all | solution.py:48
  38.4 105.5 %all-gather.5.cloned.1.call-start = ((), (), s32[]{:S(2)}) async-start(), calls=%async_computation.5 | async-start | bytes 3538944 | tf_op jit(solution)/shard_map/all_gather | solution.py:28
  39.1 151.2 %reduce-scatter.5.cloned.1.call-start = ((), (), s32[]{:S(2)}) async-start(), calls=%async_computation.7 | async-start | bytes 3538944 | tf_op jit(solution)/shard_map/reduce_scatter | solution.py:68
  143.8 5.5 %copy-start.3 = (bf16[448,4096]{1,0:T(8,128)(2,1)S(1)}, bf16[448,4096]{1,0:T(8,128)(2,1)}, u32[]{:S(2)}) copy-start(bf16[448,4096]{1,0:T(8,128)(2,1)} %reshape.97) | copy-start | bytes 11010052
  149.3 3.9 %copy-start.6 = (bf16[448,768]{1,0:T(8,128)(2,1)}, bf16[448,768]{1,0:T(8,128)(2,1)S(1)}, u32[]{:S(2)}) copy-start(bf16[448,768]{1,0:T(8,128)(2,1)S(1)} %get-tuple-element.5) | copy-start | bytes 2064388
  149.3 3.9 %copy-start.8 = (bf16[448,768]{1,0:T(8,128)(2,1)}, bf16[448,768]{1,0:T(8,128)(2,1)S(1)}, u32[]{:S(2)}) copy-start(bf16[448,768]{1,0:T(8,128)(2,1)S(1)} %get-tuple-element.6) | copy-start | bytes 2064388
  152.9 142.6 %reduce-scatter.3.cloned.1.call-start = ((), (), s32[]{:S(2)}) async-start(), calls=%async_computation.6 | async-start | bytes 7077888 | tf_op jit(solution)/shard_map/reduce_scatter | solution.py:67
  160.4 3.7 %slice-start = ((s8[6291456]{0:T(1024)(128)(4,1)}), s8[2097152]{0:T(1024)(128)(4,1)S(1)}, s32[]{:S(2)}) async-start(s8[6291456]{0:T(1024)(128)(4,1)} %bitcast.60), calls=%async_computation.8 | async-start | bytes 4194304
  160.4 3.7 %slice-start.1 = ((s8[6291456]{0:T(1024)(128)(4,1)}), s8[4194304]{0:T(1024)(128)(4,1)S(1)}, s32[]{:S(2)}) async-start(s8[6291456]{0:T(1024)(128)(4,1)} %bitcast.60), calls=%async_computation.9 | async-start | bytes 8388608
  160.4 3.8 %copy-start.7 = (bf16[448,768]{1,0:T(8,128)(2,1)S(1)}, bf16[448,768]{1,0:T(8,128)(2,1)}, u32[]{:S(2)}) copy-start(bf16[448,768]{1,0:T(8,128)(2,1)} %copy-done.6) | copy-start | bytes 2064388
  160.4 4.0 %copy-start.9 = (bf16[448,768]{1,0:T(8,128)(2,1)S(1)}, bf16[448,768]{1,0:T(8,128)(2,1)}, u32[]{:S(2)}) copy-start(bf16[448,768]{1,0:T(8,128)(2,1)} %copy-done.8) | copy-start | bytes 2064388
  174.5 102.5 %all-to-all-start.1 = ((bf16[32,14,4096]{2,1,0:T(8,128)(2,1)}), bf16[32,14,4096]{2,1,0:T(8,128)(2,1)}, u32[]{:S(2)}, u32[]{:S(2)}) async-start(bf16[32,14,4096]{2,1,0:T(8,128)(2,1)} %reshape.98), calls=%async_computation.1 | async-start | bytes 8388608 | tf_op jit(solution)/shard_map/all_to_all | solution.py:72
  285.3 1.9 copy-start
  287.4 2.4 copy-start.4
Sparse Core Ops, SparseCore 0:
  9.8 47.5 all-gather.2
  59.2 30.3 all-gather.4
  153.0 37.3 reduce-scatter.4
  192.8 46.1 reduce-scatter.2

commit v2 on v1

--- a/solution.py
+++ b/solution.py
@@ -57,6 +57,9 @@
     silu = gate_part * sigma
     hidden = (silu * up_part).astype(bf16)
     results = jnp.dot(hidden, out_full, preferred_element_type=f32).astype(bf16)
+    returned = lax.all_to_all(
+        results.reshape(experts, capacity, width), "expert", split_axis=0, concat_axis=0, tiled=True
+    ).reshape(-1, width)
     d_hidden = contract_cols(d_arrived, out_full)
     grad_down = contract_rows(hidden, d_arrived)
     d_joined = jnp.concatenate(
@@ -68,16 +71,14 @@
         lax.psum_scatter(grad_down.astype(bf16), "dp", scatter_dimension=0, tiled=True).astype(f32),
     )
     d_rows = contract_cols(d_joined, in_full).astype(bf16)
-    back = jnp.concatenate([results, d_rows], axis=1)
-    returned = lax.all_to_all(
-        back.reshape(experts, capacity, 2 * width), "expert", split_axis=0, concat_axis=0, tiled=True
-    ).reshape(-1, 2 * width)
-    picked_both = contract_rows(select, returned).reshape(tok_rows, top, 2 * width)
-    picked = picked_both[:, :, :width]
-    d_picked = picked_both[:, :, width:]
+    d_back = lax.all_to_all(
+        d_rows.reshape(experts, capacity, width), "expert", split_axis=0, concat_axis=0, tiled=True
+    ).reshape(-1, width)
+    picked = contract_rows(select, returned).reshape(tok_rows, top, width)
     mixed = jnp.einsum("tk,tkd->td", gates, picked).astype(bf16)
     d_gate = jnp.einsum("td,tkd->tk", upstream, picked)
     d_logits = gates * (d_gate - jnp.sum(gates * d_gate, axis=-1, keepdims=True))
+    d_picked = contract_rows(select, d_back).reshape(tok_rows, top, width)
     d_tokens = jnp.sum(d_picked, axis=1).astype(bf16)
     return (mixed, d_tokens, d_logits, up_share[None], down_share[None])
 

time: 309 us -> 300 us (0.971); the launches traced: 304 us -> 299 us
  waiting for transfers between devices: 183 us -> 168 us
  starting transfers between devices: 22.4 us -> 29.5 us
  matrix products: 40.7 us -> 46.9 us
    all_to_all x1 -> x2, waiting for transfers between devices: 84.8 us -> 74.8 us  [the longest x1 37.9 us: local(): lax.all_to_all(results.reshape(experts, capacity, width), 'expert', split...]
    all_to_all x1 -> x2, starting transfers between devices: 9.81 us -> 16.8 us  [the longest x1 9.56 us: local(): lax.all_to_all(results.reshape(experts, capacity, width), 'expert', split...]
    reduce_scatter x1, waiting for transfers between devices: 5.49 us -> 0.01 us  [local(): lax.psum_scatter(grad_down.astype(bf16), 'dp', scatter_dimension=0, tiled...]
    dot_general x2, matrix products: 8.46 us -> 12.9 us  [contract_cols(): lax.dot_general(left, right, (((1,), (1,)), ((), ())), preferred_element_...]
    dot_general x3 -> x4, matrix products: 14.1 us -> 16.1 us  [contract_rows(): lax.dot_general(left, right, (((0,), (0,)), ((), ())), preferred_element_...]
    reshape x2 -> x4, local copies, waits for them, and re-layouts: 10 us -> 10.5 us  [the longest x1 3.72 us: local(): returned = lax.all_to_all(results.reshape(experts, capacity, width), 'exp...]
  transfers between devices with their start and end apart: 6 -> 7, of which waited for: 3 -> 3; matrix products, arithmetic and copies ran while one was open for 23% -> 25% of each run, Pallas kernels for 0% -> 0%
where the time goes in v2:
time: 300 us; the launch traced here: 299 us
  waiting for transfers between devices  168 us (56%)
  matrix products  46.9 us (16%)
  local copies, waits for them, and re-layouts  31.8 us (11%)
  starting transfers between devices  29.5 us (10%)
  between operations  14 us (5%)
  other arithmetic  8.42 us (3%)
    all_to_all x1, waiting for transfers between devices, local(): lax.all_to_all(outgoing.reshape(experts, capacity, 2 * width), 'expert',...  91.8 us
    all_to_all x1, waiting for transfers between devices, local(): lax.all_to_all(results.reshape(experts, capacity, width), 'expert', split...  37.9 us
    all_to_all x1, waiting for transfers between devices, local(): lax.all_to_all(d_rows.reshape(experts, capacity, width), 'expert', split_...  37 us
    dot_general x4, matrix products, contract_rows(): lax.dot_general(left, right, (((0,), (0,)), ((), ())), preferred_element_...  16.1 us
    dot_general x2, matrix products, contract_cols(): lax.dot_general(left, right, (((1,), (1,)), ((), ())), preferred_element_...  12.9 us
    all_to_all x1, starting transfers between devices, local(): lax.all_to_all(outgoing.reshape(experts, capacity, 2 * width), 'expert',...  12.4 us
    all_to_all x1, starting transfers between devices, local(): lax.all_to_all(results.reshape(experts, capacity, width), 'expert', split...  9.56 us
    dot_general x1, matrix products, local(): joined = jnp.dot(piece, in_full, preferred_element_type=f32)  7.9 us
  transfers between devices with their start and end apart: 7, of which 3 were waited for; matrix products, arithmetic and copies ran while one was open for 25% of the time, Pallas kernels for 0%

profile of v2, /device:TPU:1, one launch (start us, length us, event | category | flops | bytes accessed | tf_op | source)
XLA Modules:
  0.0 298.7 jit_solution(17130487699746726111)
XLA Ops:
  7.2 0.7 all-gather.3.cloned.1.call-update
  7.9 0.8 copy.21
  8.7 0.1 reshape.113
  8.8 0.1 eq.58
  9.0 0.8 exponential_reduce_fusion
  9.8 0.1 copy.24
  9.9 0.1 div.18
  10.0 0.6 reduce-window.6
  10.6 0.2 slice_reduce_fusion
  10.9 1.7 broadcast_in_dim.23
  12.5 0.4 reshape.115
  13.0 2.1 mul.60
  15.1 2.4 mul.61
  17.6 1.8 multiply_convert_fusion
  19.4 3.0 convolution_convert_fusion.1
  22.4 5.1 %reshape.116 = bf16[32,14,4096]{2,1,0:T(8,128)(2,1)} reshape(bf16[448,4096]{1,0:T(8,128)(2,1)} %convolution_convert_fusion.1) | data formatting | bytes 7340032 | tf_op jit(solution)/shard_map/reshape | solution.py:49
  27.4 12.4 %all-to-all-start = ((bf16[32,14,4096]{2,1,0:T(8,128)(2,1)}), bf16[32,14,4096]{2,1,0:T(8,128)(2,1)}, u32[]{:S(2)}, u32[]{:S(2)}) async-start(bf16[32,14,4096]{2,1,0:T(8,128)(2,1)} %reshape.116), calls=%async_computation | async-start | bytes 8388608 | tf_op jit(solution)/shard_map/all_to_all | solution.py:48
  39.9 0.7 all-gather.5.cloned.1.call-update
  40.6 91.8 %all-to-all-done = bf16[32,14,4096]{2,1,0:T(8,128)(2,1)} async-done(((bf16[32,14,4096]{2,1,0:T(8,128)(2,1)}), bf16[32,14,4096]{2,1,0:T(8,128)(2,1)}, u32[]{:S(2)}, u32[]{:S(2)}) %all-to-all-start) | async-done | bytes 3670048 | tf_op jit(solution)/shard_map/all_to_all | solution.py:48
  132.4 5.0 %reshape.117 = bf16[448,4096]{1,0:T(8,128)(2,1)} reshape(bf16[32,14,4096]{2,1,0:T(8,128)(2,1)} %all-to-all-done) | data formatting | bytes 7340032 | tf_op jit(solution)/shard_map/reshape | solution.py:50
  137.4 7.9 %fusion.2 = f32[448,1536]{1,0:T(8,128)} fusion(bf16[1,2048,1536]{2,1,0:T(8,128)(2,1)} %all-gather.3.cloned.1.call-done, bf16[448,4096]{1,0:T(8,128)(2,1)} %reshape.117), kind=kOutput, calls=%fused_computation.3 | convolution fusion | flops 2818572288 | bytes 10878976 | tf_op jit(solution)/shard_map/dot_general | solution.py:53
  145.3 5.4 %multiply_convert_fusion.2 = (bf16[448,768]{1,0:T(8,128)(2,1)S(1)}, bf16[448,768]{1,0:T(8,128)(2,1)S(1)}, bf16[448,768]{1,0:T(8,128)(2,1)S(1)}) fusion(f32[448,1536]{1,0:T(8,128)} %fusion.2, bf16[1,768,2048]{2,1,0:T(8,128)(2,1)} %all-gather.5.cloned.1.call-done, bf16[448,4096]{1,0:T(8,128)(2,1)} %reshape.117), kind=kOutput, calls=%fused_computation.28 | convolution fusion | flops 1414447104 | bytes 9797632 | tf_op jit(solution)/shard_map/dot_general | solution.py:14
  150.8 3.5 %convolution_convert_fusion.2 = bf16[768,2048]{1,0:T(8,128)(2,1)} fusion(bf16[448,768]{1,0:T(8,128)(2,1)S(1)} %get-tuple-element.7, bf16[448,4096]{1,0:T(8,128)(2,1)S(1)} %copy-done.1), kind=kOutput, calls=%fused_computation.6 | convolution fusion | flops 1410859008 | bytes 5668864 | tf_op jit(solution)/shard_map/dot_general | solution.py:8
  154.3 0.2 reduce-scatter.3.cloned.1.call-start
  154.6 7.1 %convolution_convert_fusion = bf16[2048,1536]{1,0:T(8,128)(2,1)} fusion(bf16[448,4096]{1,0:T(8,128)(2,1)} %reshape.117, bf16[448,768]{1,0:T(8,128)(2,1)S(1)} %get-tuple-element.6, bf16[448,768]{1,0:T(8,128)(2,1)S(1)} %get-tuple-element.5), kind=kOutput, calls=%fused_computation | convolution fusion | flops 2824470528 | bytes 9502720 | tf_op jit(solution)/shard_map/dot_general | solution.py:8
  161.7 3.5 %fusion.8 = bf16[448,2048]{1,0:T(8,128)(2,1)S(1)} fusion(bf16[448,768]{1,0:T(8,128)(2,1)S(1)} %get-tuple-element.7, bf16[1,768,2048]{2,1,0:T(8,128)(2,1)} %all-gather.5.cloned.1.call-done), kind=kOutput, calls=%fused_computation.11 | convolution fusion | flops 1410203648 | bytes 5668864 | tf_op jit(solution)/shard_map/dot_general | solution.py:59
  165.2 1.6 reshape.118
  166.8 9.6 %all-to-all-start.1 = ((bf16[32,14,2048]{2,1,0:T(8,128)(2,1)}), bf16[32,14,2048]{2,1,0:T(8,128)(2,1)S(1)}, u32[]{:S(2)}, u32[]{:S(2)}) async-start(bf16[32,14,2048]{2,1,0:T(8,128)(2,1)} %reshape.118), calls=%async_computation.1 | async-start | bytes 4194304 | tf_op jit(solution)/shard_map/all_to_all | solution.py:60
  176.4 7.4 %fusion.11 = bf16[448,2048]{1,0:T(8,128)(2,1)} fusion(bf16[1,2048,1536]{2,1,0:T(8,128)(2,1)} %all-gather.3.cloned.1.call-done, bf16[448,768]{1,0:T(8,128)(2,1)} %copy-done.5, bf16[448,768]{1,0:T(8,128)(2,1)S(1)} %copy-done.4), kind=kOutput, calls=%fused_computation.12 | convolution fusion | flops 2822242304 | bytes 9502720 | tf_op jit(solution)/shard_map/dot_general | solution.py:14
  183.8 3.6 %reshape.120 = bf16[32,14,2048]{2,1,0:T(8,128)(2,1)} reshape(bf16[448,2048]{1,0:T(8,128)(2,1)} %fusion.11) | data formatting | bytes 3670016 | tf_op jit(solution)/shard_map/reshape | solution.py:75
  187.5 37.9 %all-to-all-done.1 = bf16[32,14,2048]{2,1,0:T(8,128)(2,1)S(1)} async-done(((bf16[32,14,2048]{2,1,0:T(8,128)(2,1)}), bf16[32,14,2048]{2,1,0:T(8,128)(2,1)S(1)}, u32[]{:S(2)}, u32[]{:S(2)}) %all-to-all-start.1) | async-done | bytes 1835040 | tf_op jit(solution)/shard_map/all_to_all | solution.py:60
  225.3 1.3 copy-done
  226.7 7.2 %all-to-all-start.2 = ((bf16[32,14,2048]{2,1,0:T(8,128)(2,1)}), bf16[32,14,2048]{2,1,0:T(8,128)(2,1)S(1)}, u32[]{:S(2)}, u32[]{:S(2)}) async-start(bf16[32,14,2048]{2,1,0:T(8,128)(2,1)} %reshape.120), calls=%async_computation.2 | async-start | bytes 4194304 | tf_op jit(solution)/shard_map/all_to_all | solution.py:74
  233.9 0.2 copy.27
  234.1 0.1 iota_compare_fusion
  234.2 0.2 eq.64
  234.4 0.3 copy.25
  234.7 3.7 %reshape.124 = bf16[448,2048,1]{1,0,2:T(8,128)(2,1)} reshape(bf16[32,14,2048]{2,1,0:T(8,128)(2,1)} %copy-done) | data formatting | bytes 3670016 | tf_op jit(solution)/shard_map/reshape | solution.py:62
  238.4 2.3 fusion.37
  240.7 1.3 fusion.23
  242.0 1.1 copy.41
  243.1 2.3 fusion.21
  245.5 37.0 %all-to-all-done.2 = bf16[32,14,2048]{2,1,0:T(8,128)(2,1)S(1)} async-done(((bf16[32,14,2048]{2,1,0:T(8,128)(2,1)}), bf16[32,14,2048]{2,1,0:T(8,128)(2,1)S(1)}, u32[]{:S(2)}, u32[]{:S(2)}) %all-to-all-start.2) | async-done | bytes 1835040 | tf_op jit(solution)/shard_map/all_to_all | solution.py:74
  282.5 1.5 reshape.127
  284.0 0.6 fusion.33
  284.6 3.2 %convolution_reduce_fusion = bf16[128,2048]{1,0:T(8,128)(2,1)} fusion(pred[128,2,448]{0,2,1:T(32,128)(4,1)S(1)} %copy.25, bf16[448,2048,1]{1,0,2:T(8,128)(2,1)} %reshape.127), kind=kOutput, calls=%fused_computation.25 | convolution fusion | flops 470024192 | bytes 2473984 | tf_op jit(solution)/shard_map/dot_general | solution.py:8
  287.8 1.9 bitcast_convert_fusion.2
  289.7 2.5 bitcast_convert_fusion.1
  (29 shorter events, 0.4 us)
Async XLA Ops:
  7.2 130.3 %all-gather.3.cloned.1.call-start = ((), (), s32[]{:S(2)}) async-start(), calls=%async_computation.5 | async-start | bytes 7077888 | tf_op jit(solution)/shard_map/all_gather | solution.py:27
  27.4 105.0 %all-to-all-start = ((bf16[32,14,4096]{2,1,0:T(8,128)(2,1)}), bf16[32,14,4096]{2,1,0:T(8,128)(2,1)}, u32[]{:S(2)}, u32[]{:S(2)}) async-start(bf16[32,14,4096]{2,1,0:T(8,128)(2,1)} %reshape.116), calls=%async_computation | async-start | bytes 8388608 | tf_op jit(solution)/shard_map/all_to_all | solution.py:48
  39.8 105.5 %all-gather.5.cloned.1.call-start = ((), (), s32[]{:S(2)}) async-start(), calls=%async_computation.6 | async-start | bytes 3538944 | tf_op jit(solution)/shard_map/all_gather | solution.py:28
  40.6 247.2 %reduce-scatter.5.cloned.1.call-start = ((), (), s32[]{:S(2)}) async-start(), calls=%async_computation.8 | async-start | bytes 3538944 | tf_op jit(solution)/shard_map/reduce_scatter | solution.py:71
  145.3 5.5 %copy-start.1 = (bf16[448,4096]{1,0:T(8,128)(2,1)S(1)}, bf16[448,4096]{1,0:T(8,128)(2,1)}, u32[]{:S(2)}) copy-start(bf16[448,4096]{1,0:T(8,128)(2,1)} %reshape.117) | copy-start | bytes 11010052
  150.8 3.8 %copy-start.3 = (bf16[448,768]{1,0:T(8,128)(2,1)}, bf16[448,768]{1,0:T(8,128)(2,1)S(1)}, u32[]{:S(2)}) copy-start(bf16[448,768]{1,0:T(8,128)(2,1)S(1)} %get-tuple-element.5) | copy-start | bytes 2064388
  150.8 3.8 %copy-start.5 = (bf16[448,768]{1,0:T(8,128)(2,1)}, bf16[448,768]{1,0:T(8,128)(2,1)S(1)}, u32[]{:S(2)}) copy-start(bf16[448,768]{1,0:T(8,128)(2,1)S(1)} %get-tuple-element.6) | copy-start | bytes 2064388
  154.3 135.4 %reduce-scatter.3.cloned.1.call-start = ((), (), s32[]{:S(2)}) async-start(), calls=%async_computation.7 | async-start | bytes 7077888 | tf_op jit(solution)/shard_map/reduce_scatter | solution.py:70
  166.8 9.6 %copy-start.4 = (bf16[448,768]{1,0:T(8,128)(2,1)S(1)}, bf16[448,768]{1,0:T(8,128)(2,1)}, u32[]{:S(2)}) copy-start(bf16[448,768]{1,0:T(8,128)(2,1)} %copy-done.3) | copy-start | bytes 2064388
  166.8 58.5 %all-to-all-start.1 = ((bf16[32,14,2048]{2,1,0:T(8,128)(2,1)}), bf16[32,14,2048]{2,1,0:T(8,128)(2,1)S(1)}, u32[]{:S(2)}, u32[]{:S(2)}) async-start(bf16[32,14,2048]{2,1,0:T(8,128)(2,1)} %reshape.118), calls=%async_computation.1 | async-start | bytes 4194304 | tf_op jit(solution)/shard_map/all_to_all | solution.py:60
  225.3 1.4 copy-start
  226.7 55.8 %all-to-all-start.2 = ((bf16[32,14,2048]{2,1,0:T(8,128)(2,1)}), bf16[32,14,2048]{2,1,0:T(8,128)(2,1)S(1)}, u32[]{:S(2)}, u32[]{:S(2)}) async-start(bf16[32,14,2048]{2,1,0:T(8,128)(2,1)} %reshape.120), calls=%async_computation.2 | async-start | bytes 4194304 | tf_op jit(solution)/shard_map/all_to_all | solution.py:74
  240.7 2.4 copy-start.2
Sparse Core Ops, SparseCore 0:
  9.8 47.5 all-gather.2
  59.2 30.3 all-gather.4
  154.5 37.0 reduce-scatter.4
  193.9 46.1 reduce-scatter.2

commit v3 on v2

--- a/solution.py
+++ b/solution.py
@@ -16,7 +16,13 @@
     )
 
 
-def local(tokens, cotangent, router_logits, expert_ids, w_in, w_out):
+def exchange(rows, experts, capacity, width):
+    return lax.all_to_all(
+        rows.reshape(experts, capacity, width), "expert", split_axis=0, concat_axis=0, tiled=True
+    ).reshape(-1, width)
+
+
+def body(tokens, cotangent, router_logits, expert_ids, w_in, w_out):
     f32 = jnp.float32
     bf16 = jnp.bfloat16
     tok_rows, width = tokens.shape
@@ -45,9 +51,7 @@
     d_picks = (gates[:, :, None] * upstream[:, None, :]).astype(bf16).reshape(-1, width)
     sendable = jnp.concatenate([repeated, d_picks], axis=1)
     outgoing = jnp.dot(select, sendable, preferred_element_type=f32).astype(bf16)
-    arrived = lax.all_to_all(
-        outgoing.reshape(experts, capacity, 2 * width), "expert", split_axis=0, concat_axis=0, tiled=True
-    ).reshape(-1, 2 * width)
+    arrived = exchange(outgoing, experts, capacity, 2 * width)
     piece = arrived[:, :width]
     d_arrived = arrived[:, width:]
     joined = jnp.dot(piece, in_full, preferred_element_type=f32)
@@ -57,23 +61,19 @@
     silu = gate_part * sigma
     hidden = (silu * up_part).astype(bf16)
     results = jnp.dot(hidden, out_full, preferred_element_type=f32).astype(bf16)
-    returned = lax.all_to_all(
-        results.reshape(experts, capacity, width), "expert", split_axis=0, concat_axis=0, tiled=True
-    ).reshape(-1, width)
+    returned = exchange(results, experts, capacity, width)
     d_hidden = contract_cols(d_arrived, out_full)
     grad_down = contract_rows(hidden, d_arrived)
     d_joined = jnp.concatenate(
         [d_hidden * up_part * sigma * (1.0 + gate_part * (1.0 - sigma)), d_hidden * silu], axis=1
     ).astype(bf16)
     grad_up = contract_rows(piece, d_joined)
+    d_rows = contract_cols(d_joined, in_full).astype(bf16)
     up_share, down_share = (
         lax.psum_scatter(grad_up.astype(bf16), "dp", scatter_dimension=0, tiled=True).astype(f32),
         lax.psum_scatter(grad_down.astype(bf16), "dp", scatter_dimension=0, tiled=True).astype(f32),
     )
-    d_rows = contract_cols(d_joined, in_full).astype(bf16)
-    d_back = lax.all_to_all(
-        d_rows.reshape(experts, capacity, width), "expert", split_axis=0, concat_axis=0, tiled=True
-    ).reshape(-1, width)
+    d_back = exchange(d_rows, experts, capacity, width)
     picked = contract_rows(select, returned).reshape(tok_rows, top, width)
     mixed = jnp.einsum("tk,tkd->td", gates, picked).astype(bf16)
     d_gate = jnp.einsum("td,tkd->tk", upstream, picked)
@@ -93,7 +93,7 @@
         P("expert", "dp", None),
     )
     return jax.shard_map(
-        local,
+        body,
         mesh=mesh,
         in_specs=placed,
         out_specs=(

time: 300 us -> 300 us (level)
  no operation moved by 1% of the time
where the time goes in v3:
time: 300 us; the launch traced here: 299 us
  waiting for transfers between devices  168 us (56%)
  matrix products  46.9 us (16%)
  local copies, waits for them, and re-layouts  31.9 us (11%)
  starting transfers between devices  29.5 us (10%)
  between operations  14 us (5%)
  other arithmetic  8.42 us (3%)
    all_to_all x3, waiting for transfers between devices, exchange(): lax.all_to_all(rows.reshape(experts, capacity, width), 'expert', split_ax...  167 us
    all_to_all x3, starting transfers between devices, exchange(): lax.all_to_all(rows.reshape(experts, capacity, width), 'expert', split_ax...  29.2 us
    dot_general x4, matrix products, contract_rows(): lax.dot_general(left, right, (((0,), (0,)), ((), ())), preferred_element_...  16.1 us
    dot_general x2, matrix products, contract_cols(): lax.dot_general(left, right, (((1,), (1,)), ((), ())), preferred_element_...  12.9 us
    reshape x3, local copies, waits for them, and re-layouts, exchange(): return lax.all_to_all(rows.reshape(experts, capacity, width), 'expert', s...  10.3 us
    reshape x3, local copies, waits for them, and re-layouts, exchange(): rows.reshape(experts, capacity, width)  10.3 us
    dot_general x1, matrix products, body(): joined = jnp.dot(piece, in_full, preferred_element_type=f32)  7.9 us
  transfers between devices with their start and end apart: 7, of which 3 were waited for; matrix products, arithmetic and copies ran while one was open for 25% of the time, Pallas kernels for 0%

profile of v3, /device:TPU:1, one launch (start us, length us, event | category | flops | bytes accessed | tf_op | source)
XLA Modules:
  0.0 298.7 jit_solution(17130487699746726111)
XLA Ops:
  7.2 0.7 all-gather.3.cloned.1.call-update
  7.9 0.8 copy.21
  8.7 0.1 reshape.113
  8.8 0.1 eq.58
  9.0 0.8 exponential_reduce_fusion
  9.8 0.1 copy.24
  9.9 0.1 div.18
  10.0 0.6 reduce-window.6
  10.6 0.2 slice_reduce_fusion
  10.9 1.7 broadcast_in_dim.23
  12.5 0.4 reshape.115
  13.0 2.1 mul.60
  15.1 2.4 mul.61
  17.6 1.8 multiply_convert_fusion
  19.4 3.0 convolution_convert_fusion.1
  22.4 5.1 %reshape.116 = bf16[32,14,4096]{2,1,0:T(8,128)(2,1)} reshape(bf16[448,4096]{1,0:T(8,128)(2,1)} %convolution_convert_fusion.1) | data formatting | bytes 7340032 | tf_op jit(solution)/shard_map/reshape | solution.py:21
  27.4 12.4 %all-to-all-start = ((bf16[32,14,4096]{2,1,0:T(8,128)(2,1)}), bf16[32,14,4096]{2,1,0:T(8,128)(2,1)}, u32[]{:S(2)}, u32[]{:S(2)}) async-start(bf16[32,14,4096]{2,1,0:T(8,128)(2,1)} %reshape.116), calls=%async_computation | async-start | bytes 8388608 | tf_op jit(solution)/shard_map/all_to_all | solution.py:20
  39.9 0.7 all-gather.5.cloned.1.call-update
  40.6 91.8 %all-to-all-done = bf16[32,14,4096]{2,1,0:T(8,128)(2,1)} async-done(((bf16[32,14,4096]{2,1,0:T(8,128)(2,1)}), bf16[32,14,4096]{2,1,0:T(8,128)(2,1)}, u32[]{:S(2)}, u32[]{:S(2)}) %all-to-all-start) | async-done | bytes 3670048 | tf_op jit(solution)/shard_map/all_to_all | solution.py:20
  132.4 5.0 %reshape.117 = bf16[448,4096]{1,0:T(8,128)(2,1)} reshape(bf16[32,14,4096]{2,1,0:T(8,128)(2,1)} %all-to-all-done) | data formatting | bytes 7340032 | tf_op jit(solution)/shard_map/reshape | solution.py:22
  137.4 7.9 %fusion.2 = f32[448,1536]{1,0:T(8,128)} fusion(bf16[1,2048,1536]{2,1,0:T(8,128)(2,1)} %all-gather.3.cloned.1.call-done, bf16[448,4096]{1,0:T(8,128)(2,1)} %reshape.117), kind=kOutput, calls=%fused_computation.3 | convolution fusion | flops 2818572288 | bytes 10878976 | tf_op jit(solution)/shard_map/dot_general | solution.py:57
  145.3 5.4 %multiply_convert_fusion.2 = (bf16[448,768]{1,0:T(8,128)(2,1)S(1)}, bf16[448,768]{1,0:T(8,128)(2,1)S(1)}, bf16[448,768]{1,0:T(8,128)(2,1)S(1)}) fusion(f32[448,1536]{1,0:T(8,128)} %fusion.2, bf16[1,768,2048]{2,1,0:T(8,128)(2,1)} %all-gather.5.cloned.1.call-done, bf16[448,4096]{1,0:T(8,128)(2,1)} %reshape.117), kind=kOutput, calls=%fused_computation.28 | convolution fusion | flops 1414447104 | bytes 9797632 | tf_op jit(solution)/shard_map/dot_general | solution.py:14
  150.8 3.5 %convolution_convert_fusion.2 = bf16[768,2048]{1,0:T(8,128)(2,1)} fusion(bf16[448,768]{1,0:T(8,128)(2,1)S(1)} %get-tuple-element.7, bf16[448,4096]{1,0:T(8,128)(2,1)S(1)} %copy-done.1), kind=kOutput, calls=%fused_computation.6 | convolution fusion | flops 1410859008 | bytes 5668864 | tf_op jit(solution)/shard_map/dot_general | solution.py:8
  154.3 0.2 reduce-scatter.3.cloned.1.call-start
  154.6 7.1 %convolution_convert_fusion = bf16[2048,1536]{1,0:T(8,128)(2,1)} fusion(bf16[448,4096]{1,0:T(8,128)(2,1)} %reshape.117, bf16[448,768]{1,0:T(8,128)(2,1)S(1)} %get-tuple-element.6, bf16[448,768]{1,0:T(8,128)(2,1)S(1)} %get-tuple-element.5), kind=kOutput, calls=%fused_computation | convolution fusion | flops 2824470528 | bytes 9502720 | tf_op jit(solution)/shard_map/dot_general | solution.py:8
  161.7 3.5 %fusion.8 = bf16[448,2048]{1,0:T(8,128)(2,1)S(1)} fusion(bf16[448,768]{1,0:T(8,128)(2,1)S(1)} %get-tuple-element.7, bf16[1,768,2048]{2,1,0:T(8,128)(2,1)} %all-gather.5.cloned.1.call-done), kind=kOutput, calls=%fused_computation.11 | convolution fusion | flops 1410203648 | bytes 5668864 | tf_op jit(solution)/shard_map/dot_general | solution.py:63
  165.2 1.6 reshape.118
  166.8 9.6 %all-to-all-start.1 = ((bf16[32,14,2048]{2,1,0:T(8,128)(2,1)}), bf16[32,14,2048]{2,1,0:T(8,128)(2,1)S(1)}, u32[]{:S(2)}, u32[]{:S(2)}) async-start(bf16[32,14,2048]{2,1,0:T(8,128)(2,1)} %reshape.118), calls=%async_computation.1 | async-start | bytes 4194304 | tf_op jit(solution)/shard_map/all_to_all | solution.py:20
  176.4 7.4 %fusion.11 = bf16[448,2048]{1,0:T(8,128)(2,1)} fusion(bf16[1,2048,1536]{2,1,0:T(8,128)(2,1)} %all-gather.3.cloned.1.call-done, bf16[448,768]{1,0:T(8,128)(2,1)} %copy-done.5, bf16[448,768]{1,0:T(8,128)(2,1)S(1)} %copy-done.4), kind=kOutput, calls=%fused_computation.12 | convolution fusion | flops 2822242304 | bytes 9502720 | tf_op jit(solution)/shard_map/dot_general | solution.py:14
  183.8 3.6 %reshape.120 = bf16[32,14,2048]{2,1,0:T(8,128)(2,1)} reshape(bf16[448,2048]{1,0:T(8,128)(2,1)} %fusion.11) | data formatting | bytes 3670016 | tf_op jit(solution)/shard_map/reshape | solution.py:21
  187.5 37.9 %all-to-all-done.1 = bf16[32,14,2048]{2,1,0:T(8,128)(2,1)S(1)} async-done(((bf16[32,14,2048]{2,1,0:T(8,128)(2,1)}), bf16[32,14,2048]{2,1,0:T(8,128)(2,1)S(1)}, u32[]{:S(2)}, u32[]{:S(2)}) %all-to-all-start.1) | async-done | bytes 1835040 | tf_op jit(solution)/shard_map/all_to_all | solution.py:20
  225.3 1.3 copy-done
  226.7 7.2 %all-to-all-start.2 = ((bf16[32,14,2048]{2,1,0:T(8,128)(2,1)}), bf16[32,14,2048]{2,1,0:T(8,128)(2,1)S(1)}, u32[]{:S(2)}, u32[]{:S(2)}) async-start(bf16[32,14,2048]{2,1,0:T(8,128)(2,1)} %reshape.120), calls=%async_computation.2 | async-start | bytes 4194304 | tf_op jit(solution)/shard_map/all_to_all | solution.py:20
  233.9 0.2 copy.27
  234.1 0.1 iota_compare_fusion
  234.2 0.2 eq.64
  234.4 0.3 copy.25
  234.7 3.7 %reshape.124 = bf16[448,2048,1]{1,0,2:T(8,128)(2,1)} reshape(bf16[32,14,2048]{2,1,0:T(8,128)(2,1)} %copy-done) | data formatting | bytes 3670016 | tf_op jit(solution)/shard_map/reshape | solution.py:22
  238.4 2.3 fusion.37
  240.7 1.3 fusion.23
  242.0 1.1 copy.41
  243.1 2.3 fusion.21
  245.5 37.0 %all-to-all-done.2 = bf16[32,14,2048]{2,1,0:T(8,128)(2,1)S(1)} async-done(((bf16[32,14,2048]{2,1,0:T(8,128)(2,1)}), bf16[32,14,2048]{2,1,0:T(8,128)(2,1)S(1)}, u32[]{:S(2)}, u32[]{:S(2)}) %all-to-all-start.2) | async-done | bytes 1835040 | tf_op jit(solution)/shard_map/all_to_all | solution.py:20
  282.5 1.5 reshape.127
  284.0 0.6 fusion.33
  284.6 3.2 %convolution_reduce_fusion = bf16[128,2048]{1,0:T(8,128)(2,1)} fusion(pred[128,2,448]{0,2,1:T(32,128)(4,1)S(1)} %copy.25, bf16[448,2048,1]{1,0,2:T(8,128)(2,1)} %reshape.127), kind=kOutput, calls=%fused_computation.25 | convolution fusion | flops 470024192 | bytes 2473984 | tf_op jit(solution)/shard_map/dot_general | solution.py:8
  287.8 1.9 bitcast_convert_fusion.2
  289.7 2.5 bitcast_convert_fusion.1
  (29 shorter events, 0.4 us)
Async XLA Ops:
  7.2 130.3 %all-gather.3.cloned.1.call-start = ((), (), s32[]{:S(2)}) async-start(), calls=%async_computation.5 | async-start | bytes 7077888 | tf_op jit(solution)/shard_map/all_gather | solution.py:33
  27.4 105.0 %all-to-all-start = ((bf16[32,14,4096]{2,1,0:T(8,128)(2,1)}), bf16[32,14,4096]{2,1,0:T(8,128)(2,1)}, u32[]{:S(2)}, u32[]{:S(2)}) async-start(bf16[32,14,4096]{2,1,0:T(8,128)(2,1)} %reshape.116), calls=%async_computation | async-start | bytes 8388608 | tf_op jit(solution)/shard_map/all_to_all | solution.py:20
  39.8 105.5 %all-gather.5.cloned.1.call-start = ((), (), s32[]{:S(2)}) async-start(), calls=%async_computation.6 | async-start | bytes 3538944 | tf_op jit(solution)/shard_map/all_gather | solution.py:34
  40.6 247.2 %reduce-scatter.5.cloned.1.call-start = ((), (), s32[]{:S(2)}) async-start(), calls=%async_computation.8 | async-start | bytes 3538944 | tf_op jit(solution)/shard_map/reduce_scatter | solution.py:74
  145.3 5.5 %copy-start.1 = (bf16[448,4096]{1,0:T(8,128)(2,1)S(1)}, bf16[448,4096]{1,0:T(8,128)(2,1)}, u32[]{:S(2)}) copy-start(bf16[448,4096]{1,0:T(8,128)(2,1)} %reshape.117) | copy-start | bytes 11010052
  150.8 3.8 %copy-start.3 = (bf16[448,768]{1,0:T(8,128)(2,1)}, bf16[448,768]{1,0:T(8,128)(2,1)S(1)}, u32[]{:S(2)}) copy-start(bf16[448,768]{1,0:T(8,128)(2,1)S(1)} %get-tuple-element.5) | copy-start | bytes 2064388
  150.8 3.8 %copy-start.5 = (bf16[448,768]{1,0:T(8,128)(2,1)}, bf16[448,768]{1,0:T(8,128)(2,1)S(1)}, u32[]{:S(2)}) copy-start(bf16[448,768]{1,0:T(8,128)(2,1)S(1)} %get-tuple-element.6) | copy-start | bytes 2064388
  154.3 135.4 %reduce-scatter.3.cloned.1.call-start = ((), (), s32[]{:S(2)}) async-start(), calls=%async_computation.7 | async-start | bytes 7077888 | tf_op jit(solution)/shard_map/reduce_scatter | solution.py:73
  166.8 9.6 %copy-start.4 = (bf16[448,768]{1,0:T(8,128)(2,1)S(1)}, bf16[448,768]{1,0:T(8,128)(2,1)}, u32[]{:S(2)}) copy-start(bf16[448,768]{1,0:T(8,128)(2,1)} %copy-done.3) | copy-start | bytes 2064388
  166.8 58.5 %all-to-all-start.1 = ((bf16[32,14,2048]{2,1,0:T(8,128)(2,1)}), bf16[32,14,2048]{2,1,0:T(8,128)(2,1)S(1)}, u32[]{:S(2)}, u32[]{:S(2)}) async-start(bf16[32,14,2048]{2,1,0:T(8,128)(2,1)} %reshape.118), calls=%async_computation.1 | async-start | bytes 4194304 | tf_op jit(solution)/shard_map/all_to_all | solution.py:20
  225.3 1.4 copy-start
  226.7 55.8 %all-to-all-start.2 = ((bf16[32,14,2048]{2,1,0:T(8,128)(2,1)}), bf16[32,14,2048]{2,1,0:T(8,128)(2,1)S(1)}, u32[]{:S(2)}, u32[]{:S(2)}) async-start(bf16[32,14,2048]{2,1,0:T(8,128)(2,1)} %reshape.120), calls=%async_computation.2 | async-start | bytes 4194304 | tf_op jit(solution)/shard_map/all_to_all | solution.py:20
  240.7 2.4 copy-start.2
Sparse Core Ops, SparseCore 0:
  9.8 47.5 all-gather.2
  59.2 30.3 all-gather.4
  154.5 37.0 reduce-scatter.4
  193.9 46.1 reduce-scatter.2

commit v4 on v3

--- a/solution.py
+++ b/solution.py
@@ -47,13 +47,13 @@
     diffs = router_logits[:, None, :] - router_logits[:, :, None]
     gates = 1.0 / jnp.sum(jnp.exp(diffs), axis=-1)
     upstream = cotangent.astype(f32)
+    gates, upstream = lax.optimization_barrier((gates, upstream))
     repeated = jnp.repeat(tokens, top, axis=0)
+    tok_out = jnp.dot(select, repeated, preferred_element_type=f32).astype(bf16)
+    piece = exchange(tok_out, experts, capacity, width)
     d_picks = (gates[:, :, None] * upstream[:, None, :]).astype(bf16).reshape(-1, width)
-    sendable = jnp.concatenate([repeated, d_picks], axis=1)
-    outgoing = jnp.dot(select, sendable, preferred_element_type=f32).astype(bf16)
-    arrived = exchange(outgoing, experts, capacity, 2 * width)
-    piece = arrived[:, :width]
-    d_arrived = arrived[:, width:]
+    d_out = jnp.dot(select, d_picks, preferred_element_type=f32).astype(bf16)
+    d_arrived = exchange(d_out, experts, capacity, width)
     joined = jnp.dot(piece, in_full, preferred_element_type=f32)
     gate_part = joined[:, :ff_units]
     up_part = joined[:, ff_units:]

time: 300 us -> 303 us (1.010)
  waiting for transfers between devices: 168 us -> 157 us
  local copies, waits for them, and re-layouts: 31.9 us -> 38.5 us
  matrix products: 46.9 us -> 50.9 us
  starting transfers between devices: 29.5 us -> 33.5 us
    all_to_all x3 -> x4, waiting for transfers between devices: 167 us -> 156 us  [exchange(): lax.all_to_all(rows.reshape(experts, capacity, width), 'expert', split_ax...]
    all_to_all x3 -> x4, starting transfers between devices: 29.2 us -> 33.2 us  [exchange(): lax.all_to_all(rows.reshape(experts, capacity, width), 'expert', split_ax...]
    reshape x3 -> x4, local copies, waits for them, and re-layouts: 10.3 us -> 12.5 us  [exchange(): rows.reshape(experts, capacity, width)]
    reshape x3 -> x4, local copies, waits for them, and re-layouts: 10.3 us -> 9.34 us  [exchange(): return lax.all_to_all(rows.reshape(experts, capacity, width), 'expert', s...]
  transfers between devices with their start and end apart: 7 -> 8, of which waited for: 3 -> 4; matrix products, arithmetic and copies ran while one was open for 25% -> 27% of each run, Pallas kernels for 0% -> 0%
where the time goes in v4:
time: 303 us; the launch traced here: 301 us
  waiting for transfers between devices  157 us (52%)
  matrix products  50.9 us (17%)
  local copies, waits for them, and re-layouts  38.5 us (13%)
  starting transfers between devices  33.5 us (11%)
  between operations  13.9 us (5%)
  other arithmetic  7.04 us (2%)
    all_to_all x4, waiting for transfers between devices, exchange(): lax.all_to_all(rows.reshape(experts, capacity, width), 'expert', split_ax...  156 us
    all_to_all x4, starting transfers between devices, exchange(): lax.all_to_all(rows.reshape(experts, capacity, width), 'expert', split_ax...  33.2 us
    dot_general x4, matrix products, contract_rows(): lax.dot_general(left, right, (((0,), (0,)), ((), ())), preferred_element_...  15.6 us
    dot_general x2, matrix products, contract_cols(): lax.dot_general(left, right, (((1,), (1,)), ((), ())), preferred_element_...  14.1 us
    reshape x4, local copies, waits for them, and re-layouts, exchange(): rows.reshape(experts, capacity, width)  12.5 us
    reshape x4, local copies, waits for them, and re-layouts, exchange(): return lax.all_to_all(rows.reshape(experts, capacity, width), 'expert', s...  9.34 us
    dot_general x1, matrix products, body(): joined = jnp.dot(piece, in_full, preferred_element_type=f32)  7.39 us
  transfers between devices with their start and end apart: 8, of which 4 were waited for; matrix products, arithmetic and copies ran while one was open for 27% of the time, Pallas kernels for 0%

profile of v4, /device:TPU:1, one launch (start us, length us, event | category | flops | bytes accessed | tf_op | source)
XLA Modules:
  0.0 301.1 jit_solution(16030794711030985765)
XLA Ops:
  7.2 0.7 all-gather.3.cloned.1.call-update
  7.9 0.8 copy.21
  9.0 0.6 reduce-window.6
  9.6 0.2 slice_reduce_fusion
  9.8 1.1 convert_element_type.45
  11.3 2.5 mul.65
  13.8 2.7 mul.66
  16.6 2.0 convolution_convert_fusion.2
  18.7 3.6 %reshape.121 = bf16[32,14,2048]{2,1,0:T(8,128)(2,1)} reshape(bf16[448,2048]{1,0:T(8,128)(2,1)} %convolution_convert_fusion.2) | data formatting | bytes 3670016 | tf_op jit(solution)/shard_map/reshape | solution.py:21
  22.3 12.0 %all-to-all-start.2 = ((bf16[32,14,2048]{2,1,0:T(8,128)(2,1)}), bf16[32,14,2048]{2,1,0:T(8,128)(2,1)S(1)}, u32[]{:S(2)}, u32[]{:S(2)}) async-start(bf16[32,14,2048]{2,1,0:T(8,128)(2,1)} %reshape.121), calls=%async_computation.2 | async-start | bytes 4194304 | tf_op jit(solution)/shard_map/all_to_all | solution.py:20
  34.4 0.7 all-gather.5.cloned.1.call-update
  35.1 2.7 broadcast_in_dim.23
  37.7 2.3 reshape.116
  40.0 3.1 %convolution_convert_fusion.3 = bf16[448,2048]{1,0:T(8,128)(2,1)} fusion(bf16[256,2048]{1,0:T(8,128)(2,1)} %reshape.116, s32[256]{0:T(256)S(1)} %multiply_add_fusion), kind=kOutput, calls=%fused_computation.11 | convolution fusion | flops 470794240 | bytes 2884608 | tf_op jit(solution)/shard_map/dot_general | solution.py:52
  43.1 3.6 %reshape.117 = bf16[32,14,2048]{2,1,0:T(8,128)(2,1)} reshape(bf16[448,2048]{1,0:T(8,128)(2,1)} %convolution_convert_fusion.3) | data formatting | bytes 3670016 | tf_op jit(solution)/shard_map/reshape | solution.py:21
  46.7 36.5 %all-to-all-done.2 = bf16[32,14,2048]{2,1,0:T(8,128)(2,1)S(1)} async-done(((bf16[32,14,2048]{2,1,0:T(8,128)(2,1)}), bf16[32,14,2048]{2,1,0:T(8,128)(2,1)S(1)}, u32[]{:S(2)}, u32[]{:S(2)}) %all-to-all-start.2) | async-done | bytes 1835040 | tf_op jit(solution)/shard_map/all_to_all | solution.py:20
  83.2 7.1 %all-to-all-start = ((bf16[32,14,2048]{2,1,0:T(8,128)(2,1)}), bf16[32,14,2048]{2,1,0:T(8,128)(2,1)}, u32[]{:S(2)}, u32[]{:S(2)}) async-start(bf16[32,14,2048]{2,1,0:T(8,128)(2,1)} %reshape.117), calls=%async_computation | async-start | bytes 4194304 | tf_op jit(solution)/shard_map/all_to_all | solution.py:20
  90.4 0.2 reduce-scatter.5.cloned.1.call-start
  90.6 1.5 reshape.122
  92.1 47.0 %all-to-all-done = bf16[32,14,2048]{2,1,0:T(8,128)(2,1)} async-done(((bf16[32,14,2048]{2,1,0:T(8,128)(2,1)}), bf16[32,14,2048]{2,1,0:T(8,128)(2,1)}, u32[]{:S(2)}, u32[]{:S(2)}) %all-to-all-start) | async-done | bytes 1835040 | tf_op jit(solution)/shard_map/all_to_all | solution.py:20
  139.1 2.5 reshape.118
  141.7 7.4 %fusion.2 = f32[448,1536]{1,0:T(8,128)} fusion(bf16[448,2048]{1,0:T(8,128)(2,1)S(1)} %reshape.118, bf16[1,2048,1536]{2,1,0:T(8,128)(2,1)} %all-gather.3.cloned.1.call-done), kind=kOutput, calls=%fused_computation.3 | convolution fusion | flops 2818572288 | bytes 10878976 | tf_op jit(solution)/shard_map/dot_general | solution.py:57
  149.1 6.5 %multiply_convert_fusion.2 = (bf16[448,768]{1,0:T(8,128)(2,1)}, bf16[448,768]{1,0:T(8,128)(2,1)}, bf16[448,768]{1,0:T(8,128)(2,1)S(1)}) fusion(f32[448,1536]{1,0:T(8,128)} %fusion.2, bf16[448,2048]{1,0:T(8,128)(2,1)} %reshape.122, bf16[1,768,2048]{2,1,0:T(8,128)(2,1)} %all-gather.5.cloned.1.call-done), kind=kOutput, calls=%fused_computation.22 | convolution fusion | flops 1414447104 | bytes 9797632 | tf_op jit(solution)/shard_map/dot_general | solution.py:14
  155.6 0.9 copy-done.4
  156.5 3.5 %convolution_convert_fusion.1 = bf16[768,2048]{1,0:T(8,128)(2,1)} fusion(bf16[448,768]{1,0:T(8,128)(2,1)S(1)} %get-tuple-element.11, bf16[448,2048]{1,0:T(8,128)(2,1)S(1)} %copy-done.1), kind=kOutput, calls=%fused_computation.5 | convolution fusion | flops 1410859008 | bytes 5668864 | tf_op jit(solution)/shard_map/dot_general | solution.py:8
  160.1 6.7 %convolution_convert_fusion = bf16[2048,1536]{1,0:T(8,128)(2,1)} fusion(bf16[448,2048]{1,0:T(8,128)(2,1)S(1)} %reshape.118, bf16[448,768]{1,0:T(8,128)(2,1)} %get-tuple-element.10, bf16[448,768]{1,0:T(8,128)(2,1)} %get-tuple-element.9), kind=kOutput, calls=%fused_computation | convolution fusion | flops 2824470528 | bytes 9502720 | tf_op jit(solution)/shard_map/dot_general | solution.py:8
  166.7 3.7 %fusion.8 = bf16[448,2048]{1,0:T(8,128)(2,1)S(1)} fusion(bf16[448,768]{1,0:T(8,128)(2,1)} %copy-done.4, bf16[1,768,2048]{2,1,0:T(8,128)(2,1)} %all-gather.5.cloned.1.call-done), kind=kOutput, calls=%fused_computation.12 | convolution fusion | flops 1410203648 | bytes 5668864 | tf_op jit(solution)/shard_map/dot_general | solution.py:63
  170.4 1.6 reshape.119
  172.0 7.0 %all-to-all-start.1 = ((bf16[32,14,2048]{2,1,0:T(8,128)(2,1)}), bf16[32,14,2048]{2,1,0:T(8,128)(2,1)S(1)}, u32[]{:S(2)}, u32[]{:S(2)}) async-start(bf16[32,14,2048]{2,1,0:T(8,128)(2,1)} %reshape.119), calls=%async_computation.1 | async-start | bytes 4194304 | tf_op jit(solution)/shard_map/all_to_all | solution.py:20
  179.0 7.6 %fusion.11 = bf16[448,2048]{1,0:T(8,128)(2,1)} fusion(bf16[1,2048,1536]{2,1,0:T(8,128)(2,1)} %all-gather.3.cloned.1.call-done, bf16[448,768]{1,0:T(8,128)(2,1)} %get-tuple-element.10, bf16[448,768]{1,0:T(8,128)(2,1)} %get-tuple-element.9), kind=kOutput, calls=%fused_computation.13 | convolution fusion | flops 2822242304 | bytes 9502720 | tf_op jit(solution)/shard_map/dot_general | solution.py:14
  186.7 3.6 %reshape.123 = bf16[32,14,2048]{2,1,0:T(8,128)(2,1)} reshape(bf16[448,2048]{1,0:T(8,128)(2,1)} %fusion.11) | data formatting | bytes 3670016 | tf_op jit(solution)/shard_map/reshape | solution.py:21
  190.3 37.5 %all-to-all-done.1 = bf16[32,14,2048]{2,1,0:T(8,128)(2,1)S(1)} async-done(((bf16[32,14,2048]{2,1,0:T(8,128)(2,1)}), bf16[32,14,2048]{2,1,0:T(8,128)(2,1)S(1)}, u32[]{:S(2)}, u32[]{:S(2)}) %all-to-all-start.1) | async-done | bytes 1835040 | tf_op jit(solution)/shard_map/all_to_all | solution.py:20
  227.8 1.3 copy-done
  229.1 7.0 %all-to-all-start.3 = ((bf16[32,14,2048]{2,1,0:T(8,128)(2,1)}), bf16[32,14,2048]{2,1,0:T(8,128)(2,1)S(1)}, u32[]{:S(2)}, u32[]{:S(2)}) async-start(bf16[32,14,2048]{2,1,0:T(8,128)(2,1)} %reshape.123), calls=%async_computation.3 | async-start | bytes 4194304 | tf_op jit(solution)/shard_map/all_to_all | solution.py:20
  236.3 0.2 eq.64
  236.5 0.3 copy.24
  237.0 3.8 %reshape.127 = bf16[448,2048,1]{1,0,2:T(8,128)(2,1)} reshape(bf16[32,14,2048]{2,1,0:T(8,128)(2,1)} %copy-done) | data formatting | bytes 3670016 | tf_op jit(solution)/shard_map/reshape | solution.py:22
  240.7 2.3 fusion.31
  243.0 1.0 copy-done.2
  244.0 2.4 fusion.14
  246.5 2.5 fusion.16
  249.0 1.1 copy.41
  250.1 34.8 %all-to-all-done.3 = bf16[32,14,2048]{2,1,0:T(8,128)(2,1)S(1)} async-done(((bf16[32,14,2048]{2,1,0:T(8,128)(2,1)}), bf16[32,14,2048]{2,1,0:T(8,128)(2,1)S(1)}, u32[]{:S(2)}, u32[]{:S(2)}) %all-to-all-start.3) | async-done | bytes 1835040 | tf_op jit(solution)/shard_map/all_to_all | solution.py:20
  284.8 1.5 reshape.130
  286.4 0.6 fusion.28
  287.0 3.2 %convolution_reduce_fusion = bf16[128,2048]{1,0:T(8,128)(2,1)} fusion(pred[128,2,448]{0,2,1:T(32,128)(4,1)S(1)} %copy.24, bf16[448,2048,1]{1,0,2:T(8,128)(2,1)} %reshape.130), kind=kOutput, calls=%fused_computation.19 | convolution fusion | flops 470024192 | bytes 2473984 | tf_op jit(solution)/shard_map/dot_general | solution.py:8
  290.1 1.9 bitcast_convert_fusion.2
  292.1 2.5 bitcast_convert_fusion.1
  (31 shorter events, 1.3 us)
Async XLA Ops:
  7.2 3.8 %copy-start.3 = (f32[128,2]{0,1:T(2,128)S(1)}, f32[128,2]{0,1:T(2,128)}, u32[]{:S(2)}) copy-start(f32[128,2]{0,1:T(2,128)} %param.8) | copy-start | bytes 3076
  7.2 134.5 %all-gather.3.cloned.1.call-start = ((), (), s32[]{:S(2)}) async-start(), calls=%async_computation.6 | async-start | bytes 7077888 | tf_op jit(solution)/shard_map/all_gather | solution.py:33
  22.3 60.9 %all-to-all-start.2 = ((bf16[32,14,2048]{2,1,0:T(8,128)(2,1)}), bf16[32,14,2048]{2,1,0:T(8,128)(2,1)S(1)}, u32[]{:S(2)}, u32[]{:S(2)}) async-start(bf16[32,14,2048]{2,1,0:T(8,128)(2,1)} %reshape.121), calls=%async_computation.2 | async-start | bytes 4194304 | tf_op jit(solution)/shard_map/all_to_all | solution.py:20
  34.3 114.8 %all-gather.5.cloned.1.call-start = ((), (), s32[]{:S(2)}) async-start(), calls=%async_computation.7 | async-start | bytes 3538944 | tf_op jit(solution)/shard_map/all_gather | solution.py:34
  83.2 55.9 %all-to-all-start = ((bf16[32,14,2048]{2,1,0:T(8,128)(2,1)}), bf16[32,14,2048]{2,1,0:T(8,128)(2,1)}, u32[]{:S(2)}, u32[]{:S(2)}) async-start(bf16[32,14,2048]{2,1,0:T(8,128)(2,1)} %reshape.117), calls=%async_computation | async-start | bytes 4194304 | tf_op jit(solution)/shard_map/all_to_all | solution.py:20
  90.4 199.8 %reduce-scatter.5.cloned.1.call-start = ((), (), s32[]{:S(2)}) async-start(), calls=%async_computation.9 | async-start | bytes 3538944 | tf_op jit(solution)/shard_map/reduce_scatter | solution.py:74
  149.1 7.4 %copy-start.1 = (bf16[448,2048]{1,0:T(8,128)(2,1)S(1)}, bf16[448,2048]{1,0:T(8,128)(2,1)}, u32[]{:S(2)}) copy-start(bf16[448,2048]{1,0:T(8,128)(2,1)} %reshape.122) | copy-start | bytes 5505028
  155.6 0.9 copy-start.4
  160.0 132.1 %reduce-scatter.3.cloned.1.call-start = ((), (), s32[]{:S(2)}) async-start(), calls=%async_computation.8 | async-start | bytes 7077888 | tf_op jit(solution)/shard_map/reduce_scatter | solution.py:73
  172.0 55.7 %all-to-all-start.1 = ((bf16[32,14,2048]{2,1,0:T(8,128)(2,1)}), bf16[32,14,2048]{2,1,0:T(8,128)(2,1)S(1)}, u32[]{:S(2)}, u32[]{:S(2)}) async-start(bf16[32,14,2048]{2,1,0:T(8,128)(2,1)} %reshape.119), calls=%async_computation.1 | async-start | bytes 4194304 | tf_op jit(solution)/shard_map/all_to_all | solution.py:20
  227.8 1.4 copy-start
  229.1 55.7 %all-to-all-start.3 = ((bf16[32,14,2048]{2,1,0:T(8,128)(2,1)}), bf16[32,14,2048]{2,1,0:T(8,128)(2,1)S(1)}, u32[]{:S(2)}, u32[]{:S(2)}) async-start(bf16[32,14,2048]{2,1,0:T(8,128)(2,1)} %reshape.123), calls=%async_computation.3 | async-start | bytes 4194304 | tf_op jit(solution)/shard_map/all_to_all | solution.py:20
  243.0 1.0 copy-start.2
Sparse Core Ops, SparseCore 0:
  9.8 47.5 all-gather.2
  59.2 30.3 all-gather.4
  160.1 35.2 reduce-scatter.4
  197.8 46.0 reduce-scatter.2

commit v5 on v4

--- a/solution.py
+++ b/solution.py
@@ -17,8 +17,13 @@
 
 
 def exchange(rows, experts, capacity, width):
+    lanes = 128
     return lax.all_to_all(
-        rows.reshape(experts, capacity, width), "expert", split_axis=0, concat_axis=0, tiled=True
+        rows.reshape(experts, capacity * width // lanes, lanes),
+        "expert",
+        split_axis=0,
+        concat_axis=0,
+        tiled=True,
     ).reshape(-1, width)
 
 

time: 303 us -> 281 us (0.927)
  waiting for transfers between devices: 157 us -> 134 us
    all_to_all x4, waiting for transfers between devices: 156 us -> 132 us  [exchange(): lax.all_to_all(rows.reshape(experts, capacity * width // lanes, lanes), '...]
  transfers between devices with their start and end apart: 8 -> 8, of which waited for: 4 -> 4; matrix products, arithmetic and copies ran while one was open for 27% -> 30% of each run, Pallas kernels for 0% -> 0%
where the time goes in v5:
time: 281 us; the launch traced here: 279 us
  waiting for transfers between devices  134 us (48%)
  matrix products  51 us (18%)
  local copies, waits for them, and re-layouts  40.2 us (14%)
  starting transfers between devices  33.1 us (12%)
  between operations  13.9 us (5%)
  other arithmetic  7.04 us (3%)
    all_to_all x4, waiting for transfers between devices, exchange(): lax.all_to_all(rows.reshape(experts, capacity * width // lanes, lanes), '...  132 us
    all_to_all x4, starting transfers between devices, exchange(): lax.all_to_all(rows.reshape(experts, capacity * width // lanes, lanes), '...  32.8 us
    dot_general x4, matrix products, contract_rows(): lax.dot_general(left, right, (((0,), (0,)), ((), ())), preferred_element_...  15.6 us
    dot_general x2, matrix products, contract_cols(): lax.dot_general(left, right, (((1,), (1,)), ((), ())), preferred_element_...  14.1 us
    reshape x4, local copies, waits for them, and re-layouts, exchange(): rows.reshape(experts, capacity * width // lanes, lanes)  13.5 us
    reshape x4, local copies, waits for them, and re-layouts, exchange(): return lax.all_to_all(rows.reshape(experts, capacity * width // lanes, la...  10.1 us
    dot_general x1, matrix products, body(): joined = jnp.dot(piece, in_full, preferred_element_type=f32)  7.39 us
  transfers between devices with their start and end apart: 8, of which 4 were waited for; matrix products, arithmetic and copies ran while one was open for 30% of the time, Pallas kernels for 0%

profile of v5, /device:TPU:1, one launch (start us, length us, event | category | flops | bytes accessed | tf_op | source)
XLA Modules:
  0.0 279.0 jit_solution(2958318284340279495)
XLA Ops:
  7.2 0.7 all-gather.3.cloned.1.call-update
  7.9 0.8 copy.21
  9.0 0.6 reduce-window.6
  9.6 0.2 slice_reduce_fusion
  9.8 1.1 convert_element_type.45
  11.3 2.5 mul.65
  13.8 2.7 mul.66
  16.6 2.1 convolution_convert_fusion.2
  18.7 3.9 %reshape.121 = bf16[32,224,128]{2,1,0:T(8,128)(2,1)} reshape(bf16[448,2048]{1,0:T(8,128)(2,1)} %convolution_convert_fusion.2) | data formatting | bytes 3670016 | tf_op jit(solution)/shard_map/reshape | solution.py:22
  22.6 12.0 %all-to-all-start.2 = ((bf16[32,224,128]{2,1,0:T(8,128)(2,1)}), bf16[32,224,128]{2,1,0:T(8,128)(2,1)S(1)}, u32[]{:S(2)}, u32[]{:S(2)}) async-start(bf16[32,224,128]{2,1,0:T(8,128)(2,1)} %reshape.121), calls=%async_computation.2 | async-start | bytes 3670016 | tf_op jit(solution)/shard_map/all_to_all | solution.py:21
  34.7 0.7 all-gather.5.cloned.1.call-update
  35.4 2.7 broadcast_in_dim.23
  38.0 2.3 reshape.116
  40.3 3.2 %convolution_convert_fusion.3 = bf16[448,2048]{1,0:T(8,128)(2,1)} fusion(bf16[256,2048]{1,0:T(8,128)(2,1)} %reshape.116, s32[256]{0:T(256)S(1)} %multiply_add_fusion), kind=kOutput, calls=%fused_computation.11 | convolution fusion | flops 470794240 | bytes 2884608 | tf_op jit(solution)/shard_map/dot_general | solution.py:57
  43.5 3.9 %reshape.117 = bf16[32,224,128]{2,1,0:T(8,128)(2,1)} reshape(bf16[448,2048]{1,0:T(8,128)(2,1)} %convolution_convert_fusion.3) | data formatting | bytes 3670016 | tf_op jit(solution)/shard_map/reshape | solution.py:22
  47.4 30.6 %all-to-all-done.2 = bf16[32,224,128]{2,1,0:T(8,128)(2,1)S(1)} async-done(((bf16[32,224,128]{2,1,0:T(8,128)(2,1)}), bf16[32,224,128]{2,1,0:T(8,128)(2,1)S(1)}, u32[]{:S(2)}, u32[]{:S(2)}) %all-to-all-start.2) | async-done | bytes 1835040 | tf_op jit(solution)/shard_map/all_to_all | solution.py:21
  78.0 6.7 %all-to-all-start = ((bf16[32,224,128]{2,1,0:T(8,128)(2,1)}), bf16[32,224,128]{2,1,0:T(8,128)(2,1)}, u32[]{:S(2)}, u32[]{:S(2)}) async-start(bf16[32,224,128]{2,1,0:T(8,128)(2,1)} %reshape.117), calls=%async_computation | async-start | bytes 3670016 | tf_op jit(solution)/shard_map/all_to_all | solution.py:21
  84.8 0.2 reduce-scatter.5.cloned.1.call-start
  85.0 1.8 reshape.122
  86.8 41.2 %all-to-all-done = bf16[32,224,128]{2,1,0:T(8,128)(2,1)} async-done(((bf16[32,224,128]{2,1,0:T(8,128)(2,1)}), bf16[32,224,128]{2,1,0:T(8,128)(2,1)}, u32[]{:S(2)}, u32[]{:S(2)}) %all-to-all-start) | async-done | bytes 1835040 | tf_op jit(solution)/shard_map/all_to_all | solution.py:21
  127.9 2.7 reshape.118
  130.7 7.4 %fusion.2 = f32[448,1536]{1,0:T(8,128)} fusion(bf16[448,2048]{1,0:T(8,128)(2,1)S(1)} %reshape.118, bf16[1,2048,1536]{2,1,0:T(8,128)(2,1)} %all-gather.3.cloned.1.call-done), kind=kOutput, calls=%fused_computation.3 | convolution fusion | flops 2818572288 | bytes 10878976 | tf_op jit(solution)/shard_map/dot_general | solution.py:62
  138.1 6.5 %multiply_convert_fusion.2 = (bf16[448,768]{1,0:T(8,128)(2,1)}, bf16[448,768]{1,0:T(8,128)(2,1)}, bf16[448,768]{1,0:T(8,128)(2,1)S(1)}) fusion(f32[448,1536]{1,0:T(8,128)} %fusion.2, bf16[448,2048]{1,0:T(8,128)(2,1)} %reshape.122, bf16[1,768,2048]{2,1,0:T(8,128)(2,1)} %all-gather.5.cloned.1.call-done), kind=kOutput, calls=%fused_computation.22 | convolution fusion | flops 1414447104 | bytes 9797632 | tf_op jit(solution)/shard_map/dot_general | solution.py:14
  144.6 0.9 copy-done.4
  145.4 3.5 %convolution_convert_fusion.1 = bf16[768,2048]{1,0:T(8,128)(2,1)} fusion(bf16[448,768]{1,0:T(8,128)(2,1)S(1)} %get-tuple-element.11, bf16[448,2048]{1,0:T(8,128)(2,1)S(1)} %copy-done.1), kind=kOutput, calls=%fused_computation.5 | convolution fusion | flops 1410859008 | bytes 5668864 | tf_op jit(solution)/shard_map/dot_general | solution.py:8
  149.0 6.7 %convolution_convert_fusion = bf16[2048,1536]{1,0:T(8,128)(2,1)} fusion(bf16[448,2048]{1,0:T(8,128)(2,1)S(1)} %reshape.118, bf16[448,768]{1,0:T(8,128)(2,1)} %get-tuple-element.10, bf16[448,768]{1,0:T(8,128)(2,1)} %get-tuple-element.9), kind=kOutput, calls=%fused_computation | convolution fusion | flops 2824470528 | bytes 9502720 | tf_op jit(solution)/shard_map/dot_general | solution.py:8
  155.7 3.7 %fusion.8 = bf16[448,2048]{1,0:T(8,128)(2,1)S(1)} fusion(bf16[448,768]{1,0:T(8,128)(2,1)} %copy-done.4, bf16[1,768,2048]{2,1,0:T(8,128)(2,1)} %all-gather.5.cloned.1.call-done), kind=kOutput, calls=%fused_computation.12 | convolution fusion | flops 1410203648 | bytes 5668864 | tf_op jit(solution)/shard_map/dot_general | solution.py:68
  159.4 1.8 reshape.119
  161.2 7.1 %all-to-all-start.1 = ((bf16[32,224,128]{2,1,0:T(8,128)(2,1)}), bf16[32,224,128]{2,1,0:T(8,128)(2,1)S(1)}, u32[]{:S(2)}, u32[]{:S(2)}) async-start(bf16[32,224,128]{2,1,0:T(8,128)(2,1)} %reshape.119), calls=%async_computation.1 | async-start | bytes 3670016 | tf_op jit(solution)/shard_map/all_to_all | solution.py:21
  168.3 7.6 %fusion.11 = bf16[448,2048]{1,0:T(8,128)(2,1)} fusion(bf16[1,2048,1536]{2,1,0:T(8,128)(2,1)} %all-gather.3.cloned.1.call-done, bf16[448,768]{1,0:T(8,128)(2,1)} %get-tuple-element.10, bf16[448,768]{1,0:T(8,128)(2,1)} %get-tuple-element.9), kind=kOutput, calls=%fused_computation.13 | convolution fusion | flops 2822242304 | bytes 9502720 | tf_op jit(solution)/shard_map/dot_general | solution.py:14
  175.9 3.9 %reshape.123 = bf16[32,224,128]{2,1,0:T(8,128)(2,1)} reshape(bf16[448,2048]{1,0:T(8,128)(2,1)} %fusion.11) | data formatting | bytes 3670016 | tf_op jit(solution)/shard_map/reshape | solution.py:22
  179.9 31.4 %all-to-all-done.1 = bf16[32,224,128]{2,1,0:T(8,128)(2,1)S(1)} async-done(((bf16[32,224,128]{2,1,0:T(8,128)(2,1)}), bf16[32,224,128]{2,1,0:T(8,128)(2,1)S(1)}, u32[]{:S(2)}, u32[]{:S(2)}) %all-to-all-start.1) | async-done | bytes 1835040 | tf_op jit(solution)/shard_map/all_to_all | solution.py:21
  211.3 1.3 copy-done
  212.5 6.9 %all-to-all-start.3 = ((bf16[32,224,128]{2,1,0:T(8,128)(2,1)}), bf16[32,224,128]{2,1,0:T(8,128)(2,1)S(1)}, u32[]{:S(2)}, u32[]{:S(2)}) async-start(bf16[32,224,128]{2,1,0:T(8,128)(2,1)} %reshape.123), calls=%async_computation.3 | async-start | bytes 3670016 | tf_op jit(solution)/shard_map/all_to_all | solution.py:21
  219.6 0.2 eq.64
  219.8 0.3 copy.24
  220.2 3.9 %reshape.127 = bf16[448,2048,1]{1,0,2:T(8,128)(2,1)} reshape(bf16[32,224,128]{2,1,0:T(8,128)(2,1)} %copy-done) | data formatting | bytes 3670016 | tf_op jit(solution)/shard_map/reshape | solution.py:27
  224.1 2.3 fusion.31
  226.4 1.0 copy-done.2
  227.4 2.4 fusion.14
  229.9 2.5 fusion.16
  232.4 1.1 copy.41
  233.5 29.1 %all-to-all-done.3 = bf16[32,224,128]{2,1,0:T(8,128)(2,1)S(1)} async-done(((bf16[32,224,128]{2,1,0:T(8,128)(2,1)}), bf16[32,224,128]{2,1,0:T(8,128)(2,1)S(1)}, u32[]{:S(2)}, u32[]{:S(2)}) %all-to-all-start.3) | async-done | bytes 1835040 | tf_op jit(solution)/shard_map/all_to_all | solution.py:21
  262.6 1.7 reshape.130
  264.3 0.6 fusion.28
  264.9 3.2 %convolution_reduce_fusion = bf16[128,2048]{1,0:T(8,128)(2,1)} fusion(pred[128,2,448]{0,2,1:T(32,128)(4,1)S(1)} %copy.24, bf16[448,2048,1]{1,0,2:T(8,128)(2,1)} %reshape.130), kind=kOutput, calls=%fused_computation.19 | convolution fusion | flops 470024192 | bytes 2473984 | tf_op jit(solution)/shard_map/dot_general | solution.py:8
  268.1 1.9 bitcast_convert_fusion.2
  270.0 2.5 bitcast_convert_fusion.1
  (31 shorter events, 1.3 us)
Async XLA Ops:
  7.2 3.8 %copy-start.3 = (f32[128,2]{0,1:T(2,128)S(1)}, f32[128,2]{0,1:T(2,128)}, u32[]{:S(2)}) copy-start(f32[128,2]{0,1:T(2,128)} %param.8) | copy-start | bytes 3076
  7.2 123.5 %all-gather.3.cloned.1.call-start = ((), (), s32[]{:S(2)}) async-start(), calls=%async_computation.6 | async-start | bytes 7077888 | tf_op jit(solution)/shard_map/all_gather | solution.py:38
  22.6 55.5 %all-to-all-start.2 = ((bf16[32,224,128]{2,1,0:T(8,128)(2,1)}), bf16[32,224,128]{2,1,0:T(8,128)(2,1)S(1)}, u32[]{:S(2)}, u32[]{:S(2)}) async-start(bf16[32,224,128]{2,1,0:T(8,128)(2,1)} %reshape.121), calls=%async_computation.2 | async-start | bytes 3670016 | tf_op jit(solution)/shard_map/all_to_all | solution.py:21
  34.6 103.5 %all-gather.5.cloned.1.call-start = ((), (), s32[]{:S(2)}) async-start(), calls=%async_computation.7 | async-start | bytes 3538944 | tf_op jit(solution)/shard_map/all_gather | solution.py:39
  78.0 49.9 %all-to-all-start = ((bf16[32,224,128]{2,1,0:T(8,128)(2,1)}), bf16[32,224,128]{2,1,0:T(8,128)(2,1)}, u32[]{:S(2)}, u32[]{:S(2)}) async-start(bf16[32,224,128]{2,1,0:T(8,128)(2,1)} %reshape.117), calls=%async_computation | async-start | bytes 3670016 | tf_op jit(solution)/shard_map/all_to_all | solution.py:21
  84.8 183.3 %reduce-scatter.5.cloned.1.call-start = ((), (), s32[]{:S(2)}) async-start(), calls=%async_computation.9 | async-start | bytes 3538944 | tf_op jit(solution)/shard_map/reduce_scatter | solution.py:79
  138.1 7.4 %copy-start.1 = (bf16[448,2048]{1,0:T(8,128)(2,1)S(1)}, bf16[448,2048]{1,0:T(8,128)(2,1)}, u32[]{:S(2)}) copy-start(bf16[448,2048]{1,0:T(8,128)(2,1)} %reshape.122) | copy-start | bytes 5505028
  144.6 0.9 copy-start.4
  149.0 121.1 %reduce-scatter.3.cloned.1.call-start = ((), (), s32[]{:S(2)}) async-start(), calls=%async_computation.8 | async-start | bytes 7077888 | tf_op jit(solution)/shard_map/reduce_scatter | solution.py:78
  161.2 50.1 %all-to-all-start.1 = ((bf16[32,224,128]{2,1,0:T(8,128)(2,1)}), bf16[32,224,128]{2,1,0:T(8,128)(2,1)S(1)}, u32[]{:S(2)}, u32[]{:S(2)}) async-start(bf16[32,224,128]{2,1,0:T(8,128)(2,1)} %reshape.119), calls=%async_computation.1 | async-start | bytes 3670016 | tf_op jit(solution)/shard_map/all_to_all | solution.py:21
  211.3 1.3 copy-start
  212.5 50.1 %all-to-all-start.3 = ((bf16[32,224,128]{2,1,0:T(8,128)(2,1)}), bf16[32,224,128]{2,1,0:T(8,128)(2,1)S(1)}, u32[]{:S(2)}, u32[]{:S(2)}) async-start(bf16[32,224,128]{2,1,0:T(8,128)(2,1)} %reshape.123), calls=%async_computation.3 | async-start | bytes 3670016 | tf_op jit(solution)/shard_map/all_to_all | solution.py:21
  226.4 1.0 copy-start.2
Sparse Core Ops, SparseCore 0:
  9.8 47.5 all-gather.2
  59.2 30.3 all-gather.4
  149.1 35.2 reduce-scatter.4
  186.8 46.1 reduce-scatter.2

commit v6 on v5

--- a/solution.py
+++ b/solution.py
@@ -66,6 +66,11 @@
     silu = gate_part * sigma
     hidden = (silu * up_part).astype(bf16)
     results = jnp.dot(hidden, out_full, preferred_element_type=f32).astype(bf16)
+    hidden, gate_part, up_part, results = lax.optimization_barrier(
+        (hidden, gate_part, up_part, results)
+    )
+    sigma = 1.0 / (1.0 + jnp.exp(-gate_part))
+    silu = gate_part * sigma
     returned = exchange(results, experts, capacity, width)
     d_hidden = contract_cols(d_arrived, out_full)
     grad_down = contract_rows(hidden, d_arrived)

time: 281 us -> 273 us (0.972)
  matrix products: 51 us -> 44.3 us
  local copies, waits for them, and re-layouts: 40.2 us -> 37.1 us
  transfers between devices with their start and end apart: 8 -> 8, of which waited for: 4 -> 4; matrix products, arithmetic and copies ran while one was open for 30% -> 28% of each run, Pallas kernels for 0% -> 0%
where the time goes in v6:
time: 273 us; the launch traced here: 271 us
  waiting for transfers between devices  135 us (49%)
  matrix products  44.3 us (16%)
  local copies, waits for them, and re-layouts  37.1 us (14%)
  starting transfers between devices  33.4 us (12%)
  between operations  14 us (5%)
  other arithmetic  7.97 us (3%)
    all_to_all x4, waiting for transfers between devices, exchange(): lax.all_to_all(rows.reshape(experts, capacity * width // lanes, lanes), '...  133 us
    all_to_all x4, starting transfers between devices, exchange(): lax.all_to_all(rows.reshape(experts, capacity * width // lanes, lanes), '...  33.1 us
    dot_general x4, matrix products, contract_rows(): lax.dot_general(left, right, (((0,), (0,)), ((), ())), preferred_element_...  14.5 us
    dot_general x2, matrix products, contract_cols(): lax.dot_general(left, right, (((1,), (1,)), ((), ())), preferred_element_...  12.9 us
    reshape x4, local copies, waits for them, and re-layouts, exchange(): rows.reshape(experts, capacity * width // lanes, lanes)  11.4 us
    reshape x4, local copies, waits for them, and re-layouts, exchange(): return lax.all_to_all(rows.reshape(experts, capacity * width // lanes, la...  11.3 us
    dot_general x1, matrix products, body(): joined = jnp.dot(piece, in_full, preferred_element_type=f32)  5.65 us
  transfers between devices with their start and end apart: 8, of which 4 were waited for; matrix products, arithmetic and copies ran while one was open for 28% of the time, Pallas kernels for 0%

profile of v6, /device:TPU:1, one launch (start us, length us, event | category | flops | bytes accessed | tf_op | source)
XLA Modules:
  0.0 271.3 jit_solution(15953678153630330434)
XLA Ops:
  7.2 0.7 all-gather.3.cloned.1.call-update
  7.9 0.8 copy.21
  9.0 0.6 reduce-window.6
  9.6 0.2 slice_reduce_fusion
  9.8 1.7 broadcast_in_dim.23
  11.5 0.4 reshape.116
  12.0 0.6 convolution_convert_fusion.3
  12.7 1.8 reshape.117
  14.5 12.3 %all-to-all-start = ((bf16[32,224,128]{2,1,0:T(8,128)(2,1)}), bf16[32,224,128]{2,1,0:T(8,128)(2,1)}, u32[]{:S(2)}, u32[]{:S(2)}) async-start(bf16[32,224,128]{2,1,0:T(8,128)(2,1)} %reshape.117), calls=%async_computation | async-start | bytes 3670016 | tf_op jit(solution)/shard_map/all_to_all | solution.py:21
  26.8 0.7 all-gather.5.cloned.1.call-update
  28.0 2.5 mul.68
  30.5 2.7 mul.69
  33.2 2.0 convolution_convert_fusion.2
  35.1 3.9 %reshape.121 = bf16[32,224,128]{2,1,0:T(8,128)(2,1)} reshape(bf16[448,2048]{1,0:T(8,128)(2,1)} %convolution_convert_fusion.2) | data formatting | bytes 3670016 | tf_op jit(solution)/shard_map/reshape | solution.py:22
  39.0 31.2 %all-to-all-done = bf16[32,224,128]{2,1,0:T(8,128)(2,1)} async-done(((bf16[32,224,128]{2,1,0:T(8,128)(2,1)}), bf16[32,224,128]{2,1,0:T(8,128)(2,1)}, u32[]{:S(2)}, u32[]{:S(2)}) %all-to-all-start) | async-done | bytes 1835040 | tf_op jit(solution)/shard_map/all_to_all | solution.py:21
  70.2 6.6 %all-to-all-start.2 = ((bf16[32,224,128]{2,1,0:T(8,128)(2,1)}), bf16[32,224,128]{2,1,0:T(8,128)(2,1)S(1)}, u32[]{:S(2)}, u32[]{:S(2)}) async-start(bf16[32,224,128]{2,1,0:T(8,128)(2,1)} %reshape.121), calls=%async_computation.2 | async-start | bytes 3670016 | tf_op jit(solution)/shard_map/all_to_all | solution.py:21
  76.9 3.9 %reshape.118 = bf16[448,2048]{1,0:T(8,128)(2,1)} reshape(bf16[32,224,128]{2,1,0:T(8,128)(2,1)} %all-to-all-done) | data formatting | bytes 3670016 | tf_op jit(solution)/shard_map/reshape | solution.py:27
  80.8 39.2 %all-to-all-done.2 = bf16[32,224,128]{2,1,0:T(8,128)(2,1)S(1)} async-done(((bf16[32,224,128]{2,1,0:T(8,128)(2,1)}), bf16[32,224,128]{2,1,0:T(8,128)(2,1)S(1)}, u32[]{:S(2)}, u32[]{:S(2)}) %all-to-all-start.2) | async-done | bytes 1835040 | tf_op jit(solution)/shard_map/all_to_all | solution.py:21
  120.0 1.7 reshape.122
  121.7 5.7 %fusion.2 = f32[448,1536]{1,0:T(8,128)S(1)} fusion(bf16[448,2048]{1,0:T(8,128)(2,1)} %reshape.118, bf16[1,2048,1536]{2,1,0:T(8,128)(2,1)} %all-gather.3.cloned.1.call-done), kind=kOutput, calls=%fused_computation.3 | convolution fusion | flops 2818572288 | bytes 10878976 | tf_op jit(solution)/shard_map/dot_general | solution.py:62
  127.4 2.0 fusion.30
  129.4 4.9 %fusion.8 = bf16[448,2048]{1,0:T(8,128)(2,1)} fusion(bf16[448,768]{1,0:T(8,128)(2,1)S(1)} %get-tuple-element.16, bf16[1,768,2048]{2,1,0:T(8,128)(2,1)} %all-gather.5.cloned.1.call-done), kind=kOutput, calls=%fused_computation.12 | convolution fusion | flops 1410203648 | bytes 5668864 | tf_op jit(solution)/shard_map/dot_general | solution.py:68
  134.3 3.6 %convolution_convert_fusion.1 = bf16[768,2048]{1,0:T(8,128)(2,1)} fusion(bf16[448,768]{1,0:T(8,128)(2,1)S(1)} %get-tuple-element.16, bf16[448,2048]{1,0:T(8,128)(2,1)S(1)} %copy-done.3), kind=kOutput, calls=%fused_computation.5 | convolution fusion | flops 1410859008 | bytes 5668864 | tf_op jit(solution)/shard_map/dot_general | solution.py:8
  137.9 0.2 reduce-scatter.3.cloned.1.call-start
  138.1 5.3 %multiply_convert_fusion.2 = (bf16[448,768]{1,0:T(8,128)(2,1)S(1)}, bf16[448,768]{1,0:T(8,128)(2,1)S(1)}) fusion(f32[448,768]{1,0:T(8,128)} %get-tuple-element.15, f32[448,768]{1,0:T(8,128)} %get-tuple-element.14, bf16[448,2048]{1,0:T(8,128)(2,1)} %reshape.122, bf16[1,768,2048]{2,1,0:T(8,128)(2,1)} %all-gather.5.cloned.1.call-done), kind=kOutput, calls=%fused_computation.22 | convolution fusion | flops 1413758976 | bytes 9109504 | tf_op jit(solution)/shard_map/dot_general | solution.py:14
  143.4 0.8 copy-done.6
  144.3 0.2 copy-done.7
  144.5 5.5 %convolution_convert_fusion = bf16[2048,1536]{1,0:T(8,128)(2,1)} fusion(bf16[448,2048]{1,0:T(8,128)(2,1)S(1)} %copy-done.1, bf16[448,768]{1,0:T(8,128)(2,1)S(1)} %get-tuple-element.18, bf16[448,768]{1,0:T(8,128)(2,1)S(1)} %get-tuple-element.17), kind=kOutput, calls=%fused_computation | convolution fusion | flops 2824470528 | bytes 9502720 | tf_op jit(solution)/shard_map/dot_general | solution.py:8
  150.0 1.5 copy-done.2
  151.5 1.8 reshape.119
  153.3 7.1 %all-to-all-start.1 = ((bf16[32,224,128]{2,1,0:T(8,128)(2,1)}), bf16[32,224,128]{2,1,0:T(8,128)(2,1)S(1)}, u32[]{:S(2)}, u32[]{:S(2)}) async-start(bf16[32,224,128]{2,1,0:T(8,128)(2,1)} %reshape.119), calls=%async_computation.1 | async-start | bytes 3670016 | tf_op jit(solution)/shard_map/all_to_all | solution.py:21
  160.4 7.6 %fusion.11 = bf16[448,2048]{1,0:T(8,128)(2,1)} fusion(bf16[1,2048,1536]{2,1,0:T(8,128)(2,1)} %all-gather.3.cloned.1.call-done, bf16[448,768]{1,0:T(8,128)(2,1)} %copy-done.7, bf16[448,768]{1,0:T(8,128)(2,1)} %copy-done.6), kind=kOutput, calls=%fused_computation.13 | convolution fusion | flops 2822242304 | bytes 9502720 | tf_op jit(solution)/shard_map/dot_general | solution.py:14
  168.0 3.9 %reshape.123 = bf16[32,224,128]{2,1,0:T(8,128)(2,1)} reshape(bf16[448,2048]{1,0:T(8,128)(2,1)} %fusion.11) | data formatting | bytes 3670016 | tf_op jit(solution)/shard_map/reshape | solution.py:22
  171.9 31.6 %all-to-all-done.1 = bf16[32,224,128]{2,1,0:T(8,128)(2,1)S(1)} async-done(((bf16[32,224,128]{2,1,0:T(8,128)(2,1)}), bf16[32,224,128]{2,1,0:T(8,128)(2,1)S(1)}, u32[]{:S(2)}, u32[]{:S(2)}) %all-to-all-start.1) | async-done | bytes 1835040 | tf_op jit(solution)/shard_map/all_to_all | solution.py:21
  203.6 1.2 copy-done
  204.8 7.1 %all-to-all-start.3 = ((bf16[32,224,128]{2,1,0:T(8,128)(2,1)}), bf16[32,224,128]{2,1,0:T(8,128)(2,1)S(1)}, u32[]{:S(2)}, u32[]{:S(2)}) async-start(bf16[32,224,128]{2,1,0:T(8,128)(2,1)} %reshape.123), calls=%async_computation.3 | async-start | bytes 3670016 | tf_op jit(solution)/shard_map/all_to_all | solution.py:21
  212.2 0.3 copy.24
  212.7 3.9 %reshape.127 = bf16[448,2048,1]{1,0,2:T(8,128)(2,1)} reshape(bf16[32,224,128]{2,1,0:T(8,128)(2,1)} %copy-done) | data formatting | bytes 3670016 | tf_op jit(solution)/shard_map/reshape | solution.py:27
  216.6 2.3 fusion.31
  218.9 1.3 fusion.16
  220.1 1.1 copy.41
  221.2 2.4 fusion.14
  223.7 31.2 %all-to-all-done.3 = bf16[32,224,128]{2,1,0:T(8,128)(2,1)S(1)} async-done(((bf16[32,224,128]{2,1,0:T(8,128)(2,1)}), bf16[32,224,128]{2,1,0:T(8,128)(2,1)S(1)}, u32[]{:S(2)}, u32[]{:S(2)}) %all-to-all-start.3) | async-done | bytes 1835040 | tf_op jit(solution)/shard_map/all_to_all | solution.py:21
  254.9 1.7 reshape.130
  256.6 0.6 fusion.27
  257.2 3.2 %convolution_reduce_fusion = bf16[128,2048]{1,0:T(8,128)(2,1)} fusion(pred[128,2,448]{0,2,1:T(32,128)(4,1)S(1)} %copy.24, bf16[448,2048,1]{1,0,2:T(8,128)(2,1)} %reshape.130), kind=kOutput, calls=%fused_computation.19 | convolution fusion | flops 470024192 | bytes 2473984 | tf_op jit(solution)/shard_map/dot_general | solution.py:8
  260.4 1.9 bitcast_convert_fusion.2
  262.3 2.5 bitcast_convert_fusion.1
  (38 shorter events, 1.6 us)
Async XLA Ops:
  7.2 114.6 %all-gather.3.cloned.1.call-start = ((), (), s32[]{:S(2)}) async-start(), calls=%async_computation.6 | async-start | bytes 7077888 | tf_op jit(solution)/shard_map/all_gather | solution.py:38
  14.5 13.0 %copy-start.4 = (bf16[128,2048]{1,0:T(8,128)(2,1)S(1)}, bf16[128,2048]{1,0:T(8,128)(2,1)}, u32[]{:S(2)}) copy-start(bf16[128,2048]{1,0:T(8,128)(2,1)} %param.7) | copy-start | bytes 1572868
  14.5 55.7 %all-to-all-start = ((bf16[32,224,128]{2,1,0:T(8,128)(2,1)}), bf16[32,224,128]{2,1,0:T(8,128)(2,1)}, u32[]{:S(2)}, u32[]{:S(2)}) async-start(bf16[32,224,128]{2,1,0:T(8,128)(2,1)} %reshape.117), calls=%async_computation | async-start | bytes 3670016 | tf_op jit(solution)/shard_map/all_to_all | solution.py:21
  26.8 0.9 copy-start.5
  26.8 102.6 %all-gather.5.cloned.1.call-start = ((), (), s32[]{:S(2)}) async-start(), calls=%async_computation.7 | async-start | bytes 3538944 | tf_op jit(solution)/shard_map/all_gather | solution.py:39
  70.2 49.8 %all-to-all-start.2 = ((bf16[32,224,128]{2,1,0:T(8,128)(2,1)}), bf16[32,224,128]{2,1,0:T(8,128)(2,1)S(1)}, u32[]{:S(2)}, u32[]{:S(2)}) async-start(bf16[32,224,128]{2,1,0:T(8,128)(2,1)} %reshape.121), calls=%async_computation.2 | async-start | bytes 3670016 | tf_op jit(solution)/shard_map/all_to_all | solution.py:21
  76.8 183.5 %reduce-scatter.5.cloned.1.call-start = ((), (), s32[]{:S(2)}) async-start(), calls=%async_computation.9 | async-start | bytes 3538944 | tf_op jit(solution)/shard_map/reduce_scatter | solution.py:84
  129.4 4.9 %copy-start.3 = (bf16[448,2048]{1,0:T(8,128)(2,1)S(1)}, bf16[448,2048]{1,0:T(8,128)(2,1)}, u32[]{:S(2)}) copy-start(bf16[448,2048]{1,0:T(8,128)(2,1)} %reshape.122) | copy-start | bytes 5505028
  137.9 6.6 %copy-start.1 = (bf16[448,2048]{1,0:T(8,128)(2,1)S(1)}, bf16[448,2048]{1,0:T(8,128)(2,1)}, u32[]{:S(2)}) copy-start(bf16[448,2048]{1,0:T(8,128)(2,1)} %reshape.118) | copy-start | bytes 5505028
  137.9 124.4 %reduce-scatter.3.cloned.1.call-start = ((), (), s32[]{:S(2)}) async-start(), calls=%async_computation.8 | async-start | bytes 7077888 | tf_op jit(solution)/shard_map/reduce_scatter | solution.py:83
  143.4 0.8 copy-start.6
  143.4 1.1 copy-start.7
  150.0 1.5 copy-start.2
  153.3 50.2 %all-to-all-start.1 = ((bf16[32,224,128]{2,1,0:T(8,128)(2,1)}), bf16[32,224,128]{2,1,0:T(8,128)(2,1)S(1)}, u32[]{:S(2)}, u32[]{:S(2)}) async-start(bf16[32,224,128]{2,1,0:T(8,128)(2,1)} %reshape.119), calls=%async_computation.1 | async-start | bytes 3670016 | tf_op jit(solution)/shard_map/all_to_all | solution.py:21
  203.6 1.2 copy-start
  204.8 50.1 %all-to-all-start.3 = ((bf16[32,224,128]{2,1,0:T(8,128)(2,1)}), bf16[32,224,128]{2,1,0:T(8,128)(2,1)S(1)}, u32[]{:S(2)}, u32[]{:S(2)}) async-start(bf16[32,224,128]{2,1,0:T(8,128)(2,1)} %reshape.123), calls=%async_computation.3 | async-start | bytes 3670016 | tf_op jit(solution)/shard_map/all_to_all | solution.py:21
Sparse Core Ops, SparseCore 0:
  9.8 47.5 all-gather.2
  59.2 30.3 all-gather.4
  138.0 35.2 reduce-scatter.4
  175.7 46.1 reduce-scatter.2

commit v7 on v6

--- a/solution.py
+++ b/solution.py
@@ -53,8 +53,11 @@
     gates = 1.0 / jnp.sum(jnp.exp(diffs), axis=-1)
     upstream = cotangent.astype(f32)
     gates, upstream = lax.optimization_barrier((gates, upstream))
-    repeated = jnp.repeat(tokens, top, axis=0)
-    tok_out = jnp.dot(select, repeated, preferred_element_type=f32).astype(bf16)
+    token_slot = (
+        jnp.arange(experts * capacity, dtype=jnp.int32)[:, None, None] == slot_flat.reshape(1, tok_rows, top)
+    )
+    per_token = jnp.any(token_slot, axis=2).astype(bf16)
+    tok_out = jnp.dot(per_token, tokens, preferred_element_type=f32).astype(bf16)
     piece = exchange(tok_out, experts, capacity, width)
     d_picks = (gates[:, :, None] * upstream[:, None, :]).astype(bf16).reshape(-1, width)
     d_out = jnp.dot(select, d_picks, preferred_element_type=f32).astype(bf16)
@@ -79,17 +82,18 @@
     ).astype(bf16)
     grad_up = contract_rows(piece, d_joined)
     d_rows = contract_cols(d_joined, in_full).astype(bf16)
-    up_share, down_share = (
-        lax.psum_scatter(grad_up.astype(bf16), "dp", scatter_dimension=0, tiled=True).astype(f32),
-        lax.psum_scatter(grad_down.astype(bf16), "dp", scatter_dimension=0, tiled=True).astype(f32),
+    up_part_sum, down_part_sum = (
+        lax.psum_scatter(grad_up.astype(bf16), "dp", scatter_dimension=0, tiled=True),
+        lax.psum_scatter(grad_down.astype(bf16), "dp", scatter_dimension=0, tiled=True),
     )
     d_back = exchange(d_rows, experts, capacity, width)
     picked = contract_rows(select, returned).reshape(tok_rows, top, width)
     mixed = jnp.einsum("tk,tkd->td", gates, picked).astype(bf16)
     d_gate = jnp.einsum("td,tkd->tk", upstream, picked)
     d_logits = gates * (d_gate - jnp.sum(gates * d_gate, axis=-1, keepdims=True))
-    d_picked = contract_rows(select, d_back).reshape(tok_rows, top, width)
-    d_tokens = jnp.sum(d_picked, axis=1).astype(bf16)
+    up_share = up_part_sum.astype(f32)
+    down_share = down_part_sum.astype(f32)
+    d_tokens = contract_rows(per_token, d_back).astype(bf16)
     return (mixed, d_tokens, d_logits, up_share[None], down_share[None])
 
 

time: 273 us -> 272 us (level)
  transfers between devices with their start and end apart: 8 -> 8, of which waited for: 4 -> 4; matrix products, arithmetic and copies ran while one was open for 28% -> 27% of each run, Pallas kernels for 0% -> 0%
where the time goes in v7:
time: 272 us; the launch traced here: 270 us
  waiting for transfers between devices  134 us (49%)
  matrix products  43.7 us (16%)
  local copies, waits for them, and re-layouts  35.4 us (13%)
  starting transfers between devices  33.4 us (12%)
  between operations  14 us (5%)
  other arithmetic  8.73 us (3%)
    all_to_all x4, waiting for transfers between devices, exchange(): lax.all_to_all(rows.reshape(experts, capacity * width // lanes, lanes), '...  133 us
    all_to_all x4, starting transfers between devices, exchange(): lax.all_to_all(rows.reshape(experts, capacity * width // lanes, lanes), '...  33.1 us
    dot_general x4, matrix products, contract_rows(): lax.dot_general(left, right, (((0,), (0,)), ((), ())), preferred_element_...  14.2 us
    dot_general x2, matrix products, contract_cols(): lax.dot_general(left, right, (((1,), (1,)), ((), ())), preferred_element_...  12.7 us
    reshape x4, local copies, waits for them, and re-layouts, exchange(): rows.reshape(experts, capacity * width // lanes, lanes)  11.5 us
    reshape x4, local copies, waits for them, and re-layouts, exchange(): return lax.all_to_all(rows.reshape(experts, capacity * width // lanes, la...  11.3 us
    dot_general x1, matrix products, body(): joined = jnp.dot(piece, in_full, preferred_element_type=f32)  5.65 us
  transfers between devices with their start and end apart: 8, of which 4 were waited for; matrix products, arithmetic and copies ran while one was open for 27% of the time, Pallas kernels for 0%

profile of v7, /device:TPU:1, one launch (start us, length us, event | category | flops | bytes accessed | tf_op | source)
XLA Modules:
  0.0 269.7 jit_solution(4368932122818257118)
XLA Ops:
  7.2 0.7 all-gather.3.cloned.1.call-update
  7.9 0.8 copy.31
  9.0 0.6 reduce-window.6
  9.6 0.2 slice_reduce_fusion
  10.1 0.7 multiply_add_fusion
  10.9 0.6 convolution_convert_fusion.3
  11.5 1.8 reshape.106
  13.3 12.3 %all-to-all-start = ((bf16[32,224,128]{2,1,0:T(8,128)(2,1)}), bf16[32,224,128]{2,1,0:T(8,128)(2,1)}, u32[]{:S(2)}, u32[]{:S(2)}) async-start(bf16[32,224,128]{2,1,0:T(8,128)(2,1)} %reshape.106), calls=%async_computation | async-start | bytes 3670016 | tf_op jit(solution)/shard_map/all_to_all | solution.py:21
  25.7 0.7 all-gather.5.cloned.1.call-update
  26.8 0.7 copy-done.3
  27.5 2.5 mul.76
  30.0 2.7 mul.77
  32.7 2.0 convolution_convert_fusion.2
  34.7 4.0 %reshape.110 = bf16[32,224,128]{2,1,0:T(8,128)(2,1)} reshape(bf16[448,2048]{1,0:T(8,128)(2,1)} %convolution_convert_fusion.2) | data formatting | bytes 3670016 | tf_op jit(solution)/shard_map/reshape | solution.py:22
  38.7 30.4 %all-to-all-done = bf16[32,224,128]{2,1,0:T(8,128)(2,1)} async-done(((bf16[32,224,128]{2,1,0:T(8,128)(2,1)}), bf16[32,224,128]{2,1,0:T(8,128)(2,1)}, u32[]{:S(2)}, u32[]{:S(2)}) %all-to-all-start) | async-done | bytes 1835040 | tf_op jit(solution)/shard_map/all_to_all | solution.py:21
  69.1 6.6 %all-to-all-start.2 = ((bf16[32,224,128]{2,1,0:T(8,128)(2,1)}), bf16[32,224,128]{2,1,0:T(8,128)(2,1)S(1)}, u32[]{:S(2)}, u32[]{:S(2)}) async-start(bf16[32,224,128]{2,1,0:T(8,128)(2,1)} %reshape.110), calls=%async_computation.2 | async-start | bytes 3670016 | tf_op jit(solution)/shard_map/all_to_all | solution.py:21
  75.7 3.9 %reshape.107 = bf16[448,2048]{1,0:T(8,128)(2,1)} reshape(bf16[32,224,128]{2,1,0:T(8,128)(2,1)} %all-to-all-done) | data formatting | bytes 3670016 | tf_op jit(solution)/shard_map/reshape | solution.py:27
  79.6 39.2 %all-to-all-done.2 = bf16[32,224,128]{2,1,0:T(8,128)(2,1)S(1)} async-done(((bf16[32,224,128]{2,1,0:T(8,128)(2,1)}), bf16[32,224,128]{2,1,0:T(8,128)(2,1)S(1)}, u32[]{:S(2)}, u32[]{:S(2)}) %all-to-all-start.2) | async-done | bytes 1835040 | tf_op jit(solution)/shard_map/all_to_all | solution.py:21
  118.9 1.7 reshape.111
  120.6 5.7 %fusion.2 = f32[448,1536]{1,0:T(8,128)S(1)} fusion(bf16[448,2048]{1,0:T(8,128)(2,1)} %reshape.107, bf16[1,2048,1536]{2,1,0:T(8,128)(2,1)} %all-gather.3.cloned.1.call-done), kind=kOutput, calls=%fused_computation.3 | convolution fusion | flops 2818572288 | bytes 10878976 | tf_op jit(solution)/shard_map/dot_general | solution.py:65
  126.3 2.0 fusion.32
  128.2 4.9 %fusion.8 = bf16[448,2048]{1,0:T(8,128)(2,1)} fusion(bf16[448,768]{1,0:T(8,128)(2,1)S(1)} %get-tuple-element.16, bf16[1,768,2048]{2,1,0:T(8,128)(2,1)} %all-gather.5.cloned.1.call-done), kind=kOutput, calls=%fused_computation.11 | convolution fusion | flops 1410203648 | bytes 5668864 | tf_op jit(solution)/shard_map/dot_general | solution.py:71
  133.1 3.6 %convolution_convert_fusion.1 = bf16[768,2048]{1,0:T(8,128)(2,1)} fusion(bf16[448,768]{1,0:T(8,128)(2,1)S(1)} %get-tuple-element.16, bf16[448,2048]{1,0:T(8,128)(2,1)S(1)} %copy-done.7), kind=kOutput, calls=%fused_computation.5 | convolution fusion | flops 1410859008 | bytes 5668864 | tf_op jit(solution)/shard_map/dot_general | solution.py:8
  136.7 0.2 reduce-scatter.3.cloned.1.call-start
  137.0 5.3 %multiply_convert_fusion.2 = (bf16[448,768]{1,0:T(8,128)(2,1)S(1)}, bf16[448,768]{1,0:T(8,128)(2,1)S(1)}) fusion(f32[448,768]{1,0:T(8,128)} %get-tuple-element.15, f32[448,768]{1,0:T(8,128)} %get-tuple-element.14, bf16[448,2048]{1,0:T(8,128)(2,1)} %reshape.111, bf16[1,768,2048]{2,1,0:T(8,128)(2,1)} %all-gather.5.cloned.1.call-done), kind=kOutput, calls=%fused_computation.22 | convolution fusion | flops 1413758976 | bytes 9109504 | tf_op jit(solution)/shard_map/dot_general | solution.py:14
  142.3 0.8 copy-done.10
  143.1 5.5 %convolution_convert_fusion = bf16[2048,1536]{1,0:T(8,128)(2,1)} fusion(bf16[448,2048]{1,0:T(8,128)(2,1)S(1)} %copy-done.5, bf16[448,768]{1,0:T(8,128)(2,1)S(1)} %get-tuple-element.18, bf16[448,768]{1,0:T(8,128)(2,1)S(1)} %get-tuple-element.17), kind=kOutput, calls=%fused_computation | convolution fusion | flops 2824470528 | bytes 9502720 | tf_op jit(solution)/shard_map/dot_general | solution.py:8
  148.7 1.5 copy-done.6
  150.1 1.8 reshape.108
  151.9 7.1 %all-to-all-start.1 = ((bf16[32,224,128]{2,1,0:T(8,128)(2,1)}), bf16[32,224,128]{2,1,0:T(8,128)(2,1)S(1)}, u32[]{:S(2)}, u32[]{:S(2)}) async-start(bf16[32,224,128]{2,1,0:T(8,128)(2,1)} %reshape.108), calls=%async_computation.1 | async-start | bytes 3670016 | tf_op jit(solution)/shard_map/all_to_all | solution.py:21
  159.1 7.4 %fusion.11 = bf16[448,2048]{1,0:T(8,128)(2,1)} fusion(bf16[1,2048,1536]{2,1,0:T(8,128)(2,1)} %all-gather.3.cloned.1.call-done, bf16[448,768]{1,0:T(8,128)(2,1)} %copy-done.10, bf16[448,768]{1,0:T(8,128)(2,1)S(1)} %get-tuple-element.17), kind=kOutput, calls=%fused_computation.12 | convolution fusion | flops 2822242304 | bytes 9502720 | tf_op jit(solution)/shard_map/dot_general | solution.py:14
  166.5 3.9 %reshape.112 = bf16[32,224,128]{2,1,0:T(8,128)(2,1)} reshape(bf16[448,2048]{1,0:T(8,128)(2,1)} %fusion.11) | data formatting | bytes 3670016 | tf_op jit(solution)/shard_map/reshape | solution.py:22
  170.4 31.9 %all-to-all-done.1 = bf16[32,224,128]{2,1,0:T(8,128)(2,1)S(1)} async-done(((bf16[32,224,128]{2,1,0:T(8,128)(2,1)}), bf16[32,224,128]{2,1,0:T(8,128)(2,1)S(1)}, u32[]{:S(2)}, u32[]{:S(2)}) %all-to-all-start.1) | async-done | bytes 1835040 | tf_op jit(solution)/shard_map/all_to_all | solution.py:21
  202.3 1.3 copy-done.2
  203.6 7.0 %all-to-all-start.3 = ((bf16[32,224,128]{2,1,0:T(8,128)(2,1)}), bf16[32,224,128]{2,1,0:T(8,128)(2,1)S(1)}, u32[]{:S(2)}, u32[]{:S(2)}) async-start(bf16[32,224,128]{2,1,0:T(8,128)(2,1)} %reshape.112), calls=%async_computation.3 | async-start | bytes 3670016 | tf_op jit(solution)/shard_map/all_to_all | solution.py:21
  210.8 0.2 eq.74
  211.0 0.2 copy.37
  211.1 3.9 %reshape.116 = bf16[448,2048,1]{1,0,2:T(8,128)(2,1)} reshape(bf16[32,224,128]{2,1,0:T(8,128)(2,1)} %copy-done.2) | data formatting | bytes 3670016 | tf_op jit(solution)/shard_map/reshape | solution.py:27
  215.0 2.3 fusion.20
  217.3 1.3 fusion.16
  218.5 1.1 copy.53
  219.6 2.4 fusion.14
  222.1 31.5 %all-to-all-done.3 = bf16[32,224,128]{2,1,0:T(8,128)(2,1)S(1)} async-done(((bf16[32,224,128]{2,1,0:T(8,128)(2,1)}), bf16[32,224,128]{2,1,0:T(8,128)(2,1)S(1)}, u32[]{:S(2)}, u32[]{:S(2)}) %all-to-all-start.3) | async-done | bytes 1835040 | tf_op jit(solution)/shard_map/all_to_all | solution.py:21
  253.6 1.7 reshape.113
  255.3 0.6 fusion.29
  255.9 2.8 %convolution_convert_fusion.4 = bf16[128,2048]{1,0:T(8,128)(2,1)} fusion(pred[448,128]{1,0:T(8,128)(4,1)S(1)} %fusion.22, bf16[448,2048]{1,0:T(8,128)(2,1)} %reshape.113), kind=kOutput, calls=%fused_computation.14 | convolution fusion | flops 235143168 | bytes 2416640 | tf_op jit(solution)/shard_map/dot_general | solution.py:8
  258.7 1.9 bitcast_convert_fusion.2
  260.7 2.5 bitcast_convert_fusion.1
  (45 shorter events, 1.5 us)
Async XLA Ops:
  7.2 3.7 %copy-start = (bf16[128,2048]{1,0:T(8,128)(2,1)S(1)}, bf16[128,2048]{1,0:T(8,128)(2,1)}, u32[]{:S(2)}) copy-start(bf16[128,2048]{1,0:T(8,128)(2,1)} %param.6) | copy-start | bytes 1572868
  7.2 113.4 %all-gather.3.cloned.1.call-start = ((), (), s32[]{:S(2)}) async-start(), calls=%async_computation.6 | async-start | bytes 7077888 | tf_op jit(solution)/shard_map/all_gather | solution.py:38
  13.3 13.0 %copy-start.9 = (f32[128,2]{0,1:T(2,128)S(1)}, f32[128,2]{0,1:T(2,128)}, u32[]{:S(2)}) copy-start(f32[128,2]{0,1:T(2,128)} %param.8) | copy-start | bytes 3076
  13.3 13.1 %copy-start.8 = (bf16[128,2048]{1,0:T(8,128)(2,1)S(1)}, bf16[128,2048]{1,0:T(8,128)(2,1)}, u32[]{:S(2)}) copy-start(bf16[128,2048]{1,0:T(8,128)(2,1)} %param.7) | copy-start | bytes 1572868
  13.3 55.7 %all-to-all-start = ((bf16[32,224,128]{2,1,0:T(8,128)(2,1)}), bf16[32,224,128]{2,1,0:T(8,128)(2,1)}, u32[]{:S(2)}, u32[]{:S(2)}) async-start(bf16[32,224,128]{2,1,0:T(8,128)(2,1)} %reshape.106), calls=%async_computation | async-start | bytes 3670016 | tf_op jit(solution)/shard_map/all_to_all | solution.py:21
  25.6 102.6 %all-gather.5.cloned.1.call-start = ((), (), s32[]{:S(2)}) async-start(), calls=%async_computation.7 | async-start | bytes 3538944 | tf_op jit(solution)/shard_map/all_gather | solution.py:39
  26.5 1.0 copy-start.3
  69.1 49.8 %all-to-all-start.2 = ((bf16[32,224,128]{2,1,0:T(8,128)(2,1)}), bf16[32,224,128]{2,1,0:T(8,128)(2,1)S(1)}, u32[]{:S(2)}, u32[]{:S(2)}) async-start(bf16[32,224,128]{2,1,0:T(8,128)(2,1)} %reshape.110), calls=%async_computation.2 | async-start | bytes 3670016 | tf_op jit(solution)/shard_map/all_to_all | solution.py:21
  75.7 183.1 %reduce-scatter.5.cloned.1.call-start = ((), (), s32[]{:S(2)}) async-start(), calls=%async_computation.9 | async-start | bytes 3538944 | tf_op jit(solution)/shard_map/reduce_scatter | solution.py:87
  128.2 4.9 %copy-start.7 = (bf16[448,2048]{1,0:T(8,128)(2,1)S(1)}, bf16[448,2048]{1,0:T(8,128)(2,1)}, u32[]{:S(2)}) copy-start(bf16[448,2048]{1,0:T(8,128)(2,1)} %reshape.111) | copy-start | bytes 5505028
  136.7 6.4 %copy-start.5 = (bf16[448,2048]{1,0:T(8,128)(2,1)S(1)}, bf16[448,2048]{1,0:T(8,128)(2,1)}, u32[]{:S(2)}) copy-start(bf16[448,2048]{1,0:T(8,128)(2,1)} %reshape.107) | copy-start | bytes 5505028
  136.7 124.0 %reduce-scatter.3.cloned.1.call-start = ((), (), s32[]{:S(2)}) async-start(), calls=%async_computation.8 | async-start | bytes 7077888 | tf_op jit(solution)/shard_map/reduce_scatter | solution.py:86
  142.3 0.8 copy-start.10
  148.6 1.5 copy-start.6
  151.9 50.4 %all-to-all-start.1 = ((bf16[32,224,128]{2,1,0:T(8,128)(2,1)}), bf16[32,224,128]{2,1,0:T(8,128)(2,1)S(1)}, u32[]{:S(2)}, u32[]{:S(2)}) async-start(bf16[32,224,128]{2,1,0:T(8,128)(2,1)} %reshape.108), calls=%async_computation.1 | async-start | bytes 3670016 | tf_op jit(solution)/shard_map/all_to_all | solution.py:21
  202.3 1.3 copy-start.2
  203.6 50.0 %all-to-all-start.3 = ((bf16[32,224,128]{2,1,0:T(8,128)(2,1)}), bf16[32,224,128]{2,1,0:T(8,128)(2,1)S(1)}, u32[]{:S(2)}, u32[]{:S(2)}) async-start(bf16[32,224,128]{2,1,0:T(8,128)(2,1)} %reshape.112), calls=%async_computation.3 | async-start | bytes 3670016 | tf_op jit(solution)/shard_map/all_to_all | solution.py:21
  217.3 2.4 copy-start.4
  255.9 7.3 %copy-start.1 = (bf16[128,2048]{1,0:T(8,128)(2,1)S(1)}, bf16[128,2048]{1,0:T(8,128)(2,1)}, u32[]{:S(2)}) copy-start(bf16[128,2048]{1,0:T(8,128)(2,1)} %param.6) | copy-start | bytes 1572868
Sparse Core Ops, SparseCore 0:
  9.8 47.6 all-gather.2
  59.3 30.2 all-gather.4
  136.8 35.2 reduce-scatter.4
  174.5 46.1 reduce-scatter.2

commit v8 on v7

--- a/solution.py
+++ b/solution.py
@@ -82,17 +82,26 @@
     ).astype(bf16)
     grad_up = contract_rows(piece, d_joined)
     d_rows = contract_cols(d_joined, in_full).astype(bf16)
-    up_part_sum, down_part_sum = (
-        lax.psum_scatter(grad_up.astype(bf16), "dp", scatter_dimension=0, tiled=True),
-        lax.psum_scatter(grad_down.astype(bf16), "dp", scatter_dimension=0, tiled=True),
+    replicas = lax.axis_size("dp")
+    up_size = grad_up.size // replicas
+    packed = jnp.concatenate(
+        [
+            grad_up.astype(bf16).reshape(replicas, up_size),
+            grad_down.astype(bf16).reshape(replicas, grad_down.size // replicas),
+        ],
+        axis=1,
     )
+    lanes = 128
+    summed = lax.psum_scatter(
+        packed.reshape(-1, lanes), "dp", scatter_dimension=0, tiled=True
+    ).reshape(-1)
     d_back = exchange(d_rows, experts, capacity, width)
     picked = contract_rows(select, returned).reshape(tok_rows, top, width)
     mixed = jnp.einsum("tk,tkd->td", gates, picked).astype(bf16)
     d_gate = jnp.einsum("td,tkd->tk", upstream, picked)
     d_logits = gates * (d_gate - jnp.sum(gates * d_gate, axis=-1, keepdims=True))
-    up_share = up_part_sum.astype(f32)
-    down_share = down_part_sum.astype(f32)
+    up_share = summed[:up_size].astype(f32).reshape(-1, grad_up.shape[1])
+    down_share = summed[up_size:].astype(f32).reshape(-1, grad_down.shape[1])
     d_tokens = contract_rows(per_token, d_back).astype(bf16)
     return (mixed, d_tokens, d_logits, up_share[None], down_share[None])
 

time: 272 us -> 304 us (1.12)
  local copies, waits for them, and re-layouts: 35.4 us -> 61.4 us
  other arithmetic: 8.73 us -> 16.5 us
    reshape x0 -> x3, local copies, waits for them, and re-layouts: none -> 24.9 us  [the longest x1 11.6 us: body(): packed.reshape(-1, lanes)]
    concatenate x0 -> x1, other arithmetic: none -> 10.9 us  [body(): jnp.concatenate([grad_up.astype(bf16).reshape(replicas, up_size), grad_do...]
    broadcast_in_dim x2 -> x0, other arithmetic: 4.4 us -> none  [body(): return (mixed, d_tokens, d_logits, up_share[None], down_share[None])]
  transfers between devices with their start and end apart: 8 -> 7, of which waited for: 4 -> 4; matrix products, arithmetic and copies ran while one was open for 27% -> 20% of each run, Pallas kernels for 0% -> 0%
where the time goes in v8:
time: 304 us; the launch traced here: 301 us
  waiting for transfers between devices  133 us (44%)
  local copies, waits for them, and re-layouts  61.4 us (20%)
  matrix products  43 us (14%)
  starting transfers between devices  33.2 us (11%)
  other arithmetic  16.5 us (5%)
  between operations  14 us (5%)
    all_to_all x4, waiting for transfers between devices, exchange(): lax.all_to_all(rows.reshape(experts, capacity * width // lanes, lanes), '...  132 us
    all_to_all x4, starting transfers between devices, exchange(): lax.all_to_all(rows.reshape(experts, capacity * width // lanes, lanes), '...  32.9 us
    dot_general x4, matrix products, contract_rows(): lax.dot_general(left, right, (((0,), (0,)), ((), ())), preferred_element_...  14.1 us
    dot_general x2, matrix products, contract_cols(): lax.dot_general(left, right, (((1,), (1,)), ((), ())), preferred_element_...  13.5 us
    reshape x1, local copies, waits for them, and re-layouts, body(): packed.reshape(-1, lanes)  11.6 us
    reshape x4, local copies, waits for them, and re-layouts, exchange(): rows.reshape(experts, capacity * width // lanes, lanes)  11.5 us
    reshape x4, local copies, waits for them, and re-layouts, exchange(): return lax.all_to_all(rows.reshape(experts, capacity * width // lanes, la...  11.3 us
    concatenate x1, other arithmetic, body(): jnp.concatenate([grad_up.astype(bf16).reshape(replicas, up_size), grad_do...  10.9 us
  transfers between devices with their start and end apart: 7, of which 4 were waited for; matrix products, arithmetic and copies ran while one was open for 20% of the time, Pallas kernels for 0%

profile of v8, /device:TPU:1, one launch (start us, length us, event | category | flops | bytes accessed | tf_op | source)
XLA Modules:
  0.0 301.5 jit_solution(7511347761026066812)
XLA Ops:
  7.2 0.7 all-gather.3.cloned.1.call-update
  7.9 0.8 copy.31
  9.0 0.6 reduce-window.6
  10.1 0.7 multiply_add_fusion
  10.9 0.6 convolution_convert_fusion.3
  11.5 1.8 reshape.142
  13.3 12.3 %all-to-all-start = ((bf16[32,224,128]{2,1,0:T(8,128)(2,1)}), bf16[32,224,128]{2,1,0:T(8,128)(2,1)}, u32[]{:S(2)}, u32[]{:S(2)}) async-start(bf16[32,224,128]{2,1,0:T(8,128)(2,1)} %reshape.142), calls=%async_computation | async-start | bytes 3670016 | tf_op jit(solution)/shard_map/all_to_all | solution.py:21
  25.7 0.7 all-gather.5.cloned.1.call-update
  26.8 0.7 copy-done.3
  27.5 2.5 mul.76
  30.1 2.7 mul.77
  32.8 1.9 convolution_convert_fusion.2
  34.7 4.0 %reshape.146 = bf16[32,224,128]{2,1,0:T(8,128)(2,1)} reshape(bf16[448,2048]{1,0:T(8,128)(2,1)} %convolution_convert_fusion.2) | data formatting | bytes 3670016 | tf_op jit(solution)/shard_map/reshape | solution.py:22
  38.7 30.4 %all-to-all-done = bf16[32,224,128]{2,1,0:T(8,128)(2,1)} async-done(((bf16[32,224,128]{2,1,0:T(8,128)(2,1)}), bf16[32,224,128]{2,1,0:T(8,128)(2,1)}, u32[]{:S(2)}, u32[]{:S(2)}) %all-to-all-start) | async-done | bytes 1835040 | tf_op jit(solution)/shard_map/all_to_all | solution.py:21
  69.1 6.6 %all-to-all-start.2 = ((bf16[32,224,128]{2,1,0:T(8,128)(2,1)}), bf16[32,224,128]{2,1,0:T(8,128)(2,1)S(1)}, u32[]{:S(2)}, u32[]{:S(2)}) async-start(bf16[32,224,128]{2,1,0:T(8,128)(2,1)} %reshape.146), calls=%async_computation.2 | async-start | bytes 3670016 | tf_op jit(solution)/shard_map/all_to_all | solution.py:21
  75.9 3.9 %reshape.143 = bf16[448,2048]{1,0:T(8,128)(2,1)} reshape(bf16[32,224,128]{2,1,0:T(8,128)(2,1)} %all-to-all-done) | data formatting | bytes 3670016 | tf_op jit(solution)/shard_map/reshape | solution.py:27
  79.8 39.0 %all-to-all-done.2 = bf16[32,224,128]{2,1,0:T(8,128)(2,1)S(1)} async-done(((bf16[32,224,128]{2,1,0:T(8,128)(2,1)}), bf16[32,224,128]{2,1,0:T(8,128)(2,1)S(1)}, u32[]{:S(2)}, u32[]{:S(2)}) %all-to-all-start.2) | async-done | bytes 1835040 | tf_op jit(solution)/shard_map/all_to_all | solution.py:21
  118.9 1.7 reshape.147
  120.6 5.7 %fusion.2 = f32[448,1536]{1,0:T(8,128)S(1)} fusion(bf16[448,2048]{1,0:T(8,128)(2,1)} %reshape.143, bf16[1,2048,1536]{2,1,0:T(8,128)(2,1)} %all-gather.3.cloned.1.call-done), kind=kOutput, calls=%fused_computation.4 | convolution fusion | flops 2818572288 | bytes 10878976 | tf_op jit(solution)/shard_map/dot_general | solution.py:65
  126.2 2.0 fusion.32
  128.2 3.6 %fusion.8 = bf16[448,2048]{1,0:T(8,128)(2,1)S(1)} fusion(bf16[448,768]{1,0:T(8,128)(2,1)S(1)} %get-tuple-element.16, bf16[1,768,2048]{2,1,0:T(8,128)(2,1)} %all-gather.5.cloned.1.call-done), kind=kOutput, calls=%fused_computation.12 | convolution fusion | flops 1410203648 | bytes 5668864 | tf_op jit(solution)/shard_map/dot_general | solution.py:71
  131.9 3.5 %convolution_convert_fusion.1 = bf16[768,2048]{1,0:T(8,128)(2,1)} fusion(bf16[448,768]{1,0:T(8,128)(2,1)S(1)} %get-tuple-element.16, bf16[448,2048]{1,0:T(8,128)(2,1)S(1)} %copy-done.6), kind=kOutput, calls=%fused_computation.6 | convolution fusion | flops 1410859008 | bytes 5668864 | tf_op jit(solution)/shard_map/dot_general | solution.py:8
  135.4 5.0 %reshape.151 = bf16[8,196608]{1,0:T(8,128)(2,1)} reshape(bf16[768,2048]{1,0:T(8,128)(2,1)} %convolution_convert_fusion.1) | data formatting | bytes 6291456 | tf_op jit(solution)/shard_map/reshape | solution.py:90
  140.5 5.3 %multiply_convert_fusion.2 = (bf16[448,768]{1,0:T(8,128)(2,1)S(1)}, bf16[448,768]{1,0:T(8,128)(2,1)S(1)}) fusion(f32[448,768]{1,0:T(8,128)} %get-tuple-element.15, f32[448,768]{1,0:T(8,128)} %get-tuple-element.14, bf16[448,2048]{1,0:T(8,128)(2,1)} %reshape.147, bf16[1,768,2048]{2,1,0:T(8,128)(2,1)} %all-gather.5.cloned.1.call-done), kind=kOutput, calls=%fused_computation.23 | convolution fusion | flops 1413758976 | bytes 9109504 | tf_op jit(solution)/shard_map/dot_general | solution.py:14
  145.8 0.8 copy-done.10
  146.6 5.6 %convolution_convert_fusion = bf16[2048,1536]{1,0:T(8,128)(2,1)} fusion(bf16[448,2048]{1,0:T(8,128)(2,1)S(1)} %copy-done.5, bf16[448,768]{1,0:T(8,128)(2,1)S(1)} %get-tuple-element.18, bf16[448,768]{1,0:T(8,128)(2,1)S(1)} %get-tuple-element.17), kind=kOutput, calls=%fused_computation.1 | convolution fusion | flops 2824470528 | bytes 9502720 | tf_op jit(solution)/shard_map/dot_general | solution.py:8
  152.2 8.3 %reshape.150 = bf16[8,393216]{1,0:T(8,128)(2,1)} reshape(bf16[2048,1536]{1,0:T(8,128)(2,1)} %convolution_convert_fusion) | data formatting | bytes 12582912 | tf_op jit(solution)/shard_map/reshape | solution.py:89
  160.5 10.9 %pad_maximum_fusion = bf16[8,589824]{1,0:T(8,128)(2,1)} fusion(bf16[8,196608]{1,0:T(8,128)(2,1)} %reshape.151, bf16[8,393216]{1,0:T(8,128)(2,1)} %reshape.150), kind=kLoop, calls=%fused_computation | loop fusion | flops 18874368 | bytes 18874368 | tf_op jit(solution)/shard_map/concatenate | solution.py:87
  171.4 11.6 %reshape.152 = bf16[36864,128]{1,0:T(8,128)(2,1)} reshape(bf16[8,589824]{1,0:T(8,128)(2,1)} %pad_maximum_fusion) | data formatting | bytes 18874368 | tf_op jit(solution)/shard_map/reshape | solution.py:96
  183.0 1.8 reshape.144
  184.8 7.2 %all-to-all-start.1 = ((bf16[32,224,128]{2,1,0:T(8,128)(2,1)}), bf16[32,224,128]{2,1,0:T(8,128)(2,1)S(1)}, u32[]{:S(2)}, u32[]{:S(2)}) async-start(bf16[32,224,128]{2,1,0:T(8,128)(2,1)} %reshape.144), calls=%async_computation.1 | async-start | bytes 3670016 | tf_op jit(solution)/shard_map/all_to_all | solution.py:21
  192.0 8.1 %fusion.11 = bf16[448,2048]{1,0:T(8,128)(2,1)} fusion(bf16[1,2048,1536]{2,1,0:T(8,128)(2,1)} %all-gather.3.cloned.1.call-done, bf16[448,768]{1,0:T(8,128)(2,1)} %copy-done.10, bf16[448,768]{1,0:T(8,128)(2,1)S(1)} %get-tuple-element.17), kind=kOutput, calls=%fused_computation.13 | convolution fusion | flops 2822242304 | bytes 9502720 | tf_op jit(solution)/shard_map/dot_general | solution.py:14
  200.1 3.9 %reshape.148 = bf16[32,224,128]{2,1,0:T(8,128)(2,1)} reshape(bf16[448,2048]{1,0:T(8,128)(2,1)} %fusion.11) | data formatting | bytes 3670016 | tf_op jit(solution)/shard_map/reshape | solution.py:22
  204.1 30.8 %all-to-all-done.1 = bf16[32,224,128]{2,1,0:T(8,128)(2,1)S(1)} async-done(((bf16[32,224,128]{2,1,0:T(8,128)(2,1)}), bf16[32,224,128]{2,1,0:T(8,128)(2,1)S(1)}, u32[]{:S(2)}, u32[]{:S(2)}) %all-to-all-start.1) | async-done | bytes 1835040 | tf_op jit(solution)/shard_map/all_to_all | solution.py:21
  234.9 1.3 copy-done.2
  236.2 6.9 %all-to-all-start.3 = ((bf16[32,224,128]{2,1,0:T(8,128)(2,1)}), bf16[32,224,128]{2,1,0:T(8,128)(2,1)S(1)}, u32[]{:S(2)}, u32[]{:S(2)}) async-start(bf16[32,224,128]{2,1,0:T(8,128)(2,1)} %reshape.148), calls=%async_computation.3 | async-start | bytes 3670016 | tf_op jit(solution)/shard_map/all_to_all | solution.py:21
  243.6 3.9 %reshape.155 = bf16[448,2048,1]{1,0,2:T(8,128)(2,1)} reshape(bf16[32,224,128]{2,1,0:T(8,128)(2,1)} %copy-done.2) | data formatting | bytes 3670016 | tf_op jit(solution)/shard_map/reshape | solution.py:27
  247.5 2.2 fusion.20
  249.7 1.3 fusion.16
  251.0 1.1 copy.53
  252.1 2.4 fusion.14
  254.5 31.7 %all-to-all-done.3 = bf16[32,224,128]{2,1,0:T(8,128)(2,1)S(1)} async-done(((bf16[32,224,128]{2,1,0:T(8,128)(2,1)}), bf16[32,224,128]{2,1,0:T(8,128)(2,1)S(1)}, u32[]{:S(2)}, u32[]{:S(2)}) %all-to-all-start.3) | async-done | bytes 1835040 | tf_op jit(solution)/shard_map/all_to_all | solution.py:21
  286.2 1.7 reshape.149
  288.0 0.6 fusion.29
  288.5 2.8 convolution_convert_fusion.4
  291.3 1.1 slice_convert_fusion.1
  292.5 1.0 reshape.154
  293.6 1.4 reshape.153
  (48 shorter events, 2.3 us)
Async XLA Ops:
  7.2 3.7 %copy-start = (bf16[128,2048]{1,0:T(8,128)(2,1)S(1)}, bf16[128,2048]{1,0:T(8,128)(2,1)}, u32[]{:S(2)}) copy-start(bf16[128,2048]{1,0:T(8,128)(2,1)} %param.6) | copy-start | bytes 1572868
  7.2 113.4 %all-gather.3.cloned.1.call-start = ((), (), s32[]{:S(2)}) async-start(), calls=%async_computation.5 | async-start | bytes 7077888 | tf_op jit(solution)/shard_map/all_gather | solution.py:38
  13.3 13.0 %copy-start.9 = (f32[128,2]{0,1:T(2,128)S(1)}, f32[128,2]{0,1:T(2,128)}, u32[]{:S(2)}) copy-start(f32[128,2]{0,1:T(2,128)} %param.8) | copy-start | bytes 3076
  13.3 13.1 %copy-start.8 = (bf16[128,2048]{1,0:T(8,128)(2,1)S(1)}, bf16[128,2048]{1,0:T(8,128)(2,1)}, u32[]{:S(2)}) copy-start(bf16[128,2048]{1,0:T(8,128)(2,1)} %param.7) | copy-start | bytes 1572868
  13.3 55.7 %all-to-all-start = ((bf16[32,224,128]{2,1,0:T(8,128)(2,1)}), bf16[32,224,128]{2,1,0:T(8,128)(2,1)}, u32[]{:S(2)}, u32[]{:S(2)}) async-start(bf16[32,224,128]{2,1,0:T(8,128)(2,1)} %reshape.142), calls=%async_computation | async-start | bytes 3670016 | tf_op jit(solution)/shard_map/all_to_all | solution.py:21
  25.6 102.6 %all-gather.5.cloned.1.call-start = ((), (), s32[]{:S(2)}) async-start(), calls=%async_computation.6 | async-start | bytes 3538944 | tf_op jit(solution)/shard_map/all_gather | solution.py:39
  26.5 1.0 copy-start.3
  69.1 49.8 %all-to-all-start.2 = ((bf16[32,224,128]{2,1,0:T(8,128)(2,1)}), bf16[32,224,128]{2,1,0:T(8,128)(2,1)S(1)}, u32[]{:S(2)}, u32[]{:S(2)}) async-start(bf16[32,224,128]{2,1,0:T(8,128)(2,1)} %reshape.146), calls=%async_computation.2 | async-start | bytes 3670016 | tf_op jit(solution)/shard_map/all_to_all | solution.py:21
  75.7 215.6 %reduce-scatter.2.cloned.1.call-start = ((), (), s32[]{:S(2)}) async-start(), calls=%async_computation.7 | async-start | bytes 10616832 | tf_op jit(solution)/shard_map/reduce_scatter | solution.py:95
  128.2 3.6 %copy-start.6 = (bf16[448,2048]{1,0:T(8,128)(2,1)S(1)}, bf16[448,2048]{1,0:T(8,128)(2,1)}, u32[]{:S(2)}) copy-start(bf16[448,2048]{1,0:T(8,128)(2,1)} %reshape.147) | copy-start | bytes 5505028
  140.5 6.2 %copy-start.5 = (bf16[448,2048]{1,0:T(8,128)(2,1)S(1)}, bf16[448,2048]{1,0:T(8,128)(2,1)}, u32[]{:S(2)}) copy-start(bf16[448,2048]{1,0:T(8,128)(2,1)} %reshape.143) | copy-start | bytes 5505028
  145.8 0.8 copy-start.10
  184.8 50.1 %all-to-all-start.1 = ((bf16[32,224,128]{2,1,0:T(8,128)(2,1)}), bf16[32,224,128]{2,1,0:T(8,128)(2,1)S(1)}, u32[]{:S(2)}, u32[]{:S(2)}) async-start(bf16[32,224,128]{2,1,0:T(8,128)(2,1)} %reshape.144), calls=%async_computation.1 | async-start | bytes 3670016 | tf_op jit(solution)/shard_map/all_to_all | solution.py:21
  234.9 1.3 copy-start.2
  236.2 50.1 %all-to-all-start.3 = ((bf16[32,224,128]{2,1,0:T(8,128)(2,1)}), bf16[32,224,128]{2,1,0:T(8,128)(2,1)S(1)}, u32[]{:S(2)}, u32[]{:S(2)}) async-start(bf16[32,224,128]{2,1,0:T(8,128)(2,1)} %reshape.148), calls=%async_computation.3 | async-start | bytes 3670016 | tf_op jit(solution)/shard_map/all_to_all | solution.py:21
  249.7 2.4 copy-start.4
  291.3 2.2 copy-start.7
  293.5 1.5 copy-start.1
Sparse Core Ops, SparseCore 0:
  9.8 47.6 all-gather.2
  59.3 30.2 all-gather.4
  183.1 58.5 reduce-scatter.1
